TPU v7x, 32 devices: a whole 2x2x4 slice. The times are simulated.
32 devices in a mesh: tile: 8 (over y, x, core), dir: 4 (over z).
Axes of the slice: x: 2, y: 2, z: 4, core: 2. Of those that a mesh axis runs over, the one named last changes fastest.
Arguments:
- screens: bfloat16 [6, 512, 2048], P(None, 'tile'), may hold values from -13 to 13
- ray_shift: int32 [16, 6, 2], P('dir'), may hold values from -128 to 2047, as said below
- ray_weight: float32 [16, 6, 4], P('dir'), may hold values from 0 to 0.5
- influence_index: int32 [512, 16, 16], P('tile', 'dir'), may hold values from 0 to 69, as said below
- influence: bfloat16 [512, 16, 16, 128], P('tile', 'dir'), may hold values from 0 to 0.22
- pupil_mask: int32 [512, 2048], P('tile', 'dir'), may hold values 0 or 1
- petal: int32 [24, 48], P('tile', 'dir'), may hold values from 0 to 6
Outputs:
- commands: float32 [24, 48], P('tile', 'dir')
- corrected: bfloat16 [16, 512, 2048], P('dir', 'tile')
Inputs may be any that keep to these rules, and one draw needn't show every extreme that they name: ray_shift[..., 0], the row offset, lies in -128 to 127 and reaches both ends; ray_shift[..., 1], the column offset, lies in 0 to 2047. `influence_index`: each entry names a grid point of the tile's own actuator block extended by one actuator on each side, flattened row by row with 14 points a row; entries may repeat.
All inputs are finite; a program needn't handle non-finite values. No bound on the sum of `pupil_mask` on one device may be relied on, other than what follows from the above.
Results may differ from a plain program's by a relative error of at most 0.007.
Values may be sent and summed in bfloat16 or wider, within the bound.
No kernel may reach another device: no remote copies, remote signals or barrier semaphores. Data moves between devices by JAX's collectives and lax.ppermute only.
A program may use at most 128 MiB of HBM per device.

v0:
```python
import jax
import numpy as np
import jax.numpy as jnp
from jax import lax
from jax.experimental import pallas as pl
from jax.experimental.pallas import tpu as pltpu
from jax.sharding import PartitionSpec as P

SPAN = 2
AR_DEV = 3
AC_DEV = 12
ITERS = 3


ridge_weight = 1.0
piston_weight = 0.002
highest = lax.Precision.HIGHEST


def passed_along(array, axis, by):
    size = lax.axis_size(axis)
    return lax.ppermute(array, axis, [(i, (i + by) % size) for i in range(size)])


def band_stack_whole(piece):
    bands = []
    for offset in range(SPAN, -SPAN - 1, -1):
        if offset == 0:
            bands.append(piece)
        else:
            bands.append(passed_along(piece, "tile", offset))
    return jnp.concatenate(bands, axis=1)


def trace_kernel(shift_ref, gain_ref, rim_ref, phase_ref):
    member = pl.program_id(0)
    layers, rim_rows, columns = rim_ref.shape
    band_rows = phase_ref.shape[1]
    rim_depth = (rim_rows - band_rows) // 2
    chunk_rows = band_rows + 16
    total = jnp.zeros((band_rows, columns), jnp.float32)
    row_index = lax.broadcasted_iota(jnp.int32, (band_rows, chunk_rows), 0)
    chunk_index = lax.broadcasted_iota(jnp.int32, (band_rows, chunk_rows), 1)
    for layer_index in range(layers):
        first = rim_depth + shift_ref[member, layer_index, 0]
        start = jnp.clip((first // 16) * 16, 0, rim_rows - chunk_rows)
        start = pl.multiple_of(start, 16)
        lead = first - start
        chunk = rim_ref[layer_index, pl.ds(start, chunk_rows), :].astype(jnp.float32)
        turn = (columns - lax.rem(shift_ref[member, layer_index, 1], columns)) % columns
        window = pltpu.roll(chunk, turn, 1)
        beside = pltpu.roll(window, columns - 1, 1)
        upper = (chunk_index == row_index + lead).astype(jnp.bfloat16)
        lower = (chunk_index == row_index + lead + 1).astype(jnp.bfloat16)
        window = window.astype(jnp.bfloat16)
        beside = beside.astype(jnp.bfloat16)
        top = jnp.dot(upper, window, preferred_element_type=jnp.float32)
        top_beside = jnp.dot(upper, beside, preferred_element_type=jnp.float32)
        bottom = jnp.dot(lower, window, preferred_element_type=jnp.float32)
        bottom_beside = jnp.dot(lower, beside, preferred_element_type=jnp.float32)
        total = total + (
            gain_ref[member, layer_index, 0] * top
            + gain_ref[member, layer_index, 1] * top_beside
            + gain_ref[member, layer_index, 2] * bottom
            + gain_ref[member, layer_index, 3] * bottom_beside
        )
    phase_ref[0] = total


def trace_all(padded_rim, ray_shift, ray_weight, band_rows):
    layers, rim_rows, columns = padded_rim.shape
    members = ray_shift.shape[0]
    return pl.pallas_call(
        trace_kernel,
        out_shape=jax.ShapeDtypeStruct((members, band_rows, columns), jnp.float32),
        grid=(members,),
        in_specs=[
            pl.BlockSpec(memory_space=pltpu.SMEM),
            pl.BlockSpec(memory_space=pltpu.SMEM),
            pl.BlockSpec((layers, rim_rows, columns), lambda m: (0, 0, 0)),
        ],
        out_specs=pl.BlockSpec((1, band_rows, columns), lambda m: (m, 0, 0)),
        compiler_params=pltpu.CompilerParams(vmem_limit_bytes=48 * 1024 * 1024),
    )(ray_shift, ray_weight, padded_rim)


def windows(array, axis, count, stride, width):
    parts = [
        lax.slice_in_dim(array, offset, offset + stride * (count - 1) + 1, stride=stride, axis=axis)
        for offset in range(width)
    ]
    return jnp.stack(parts, axis=axis + 1)


def on_device(screens, ray_shift, ray_weight, influence_index, influence, pupil_mask, petal):
    band_rows = screens.shape[1]
    padded_rim = band_stack_whole(screens)
    phases = trace_all(padded_rim, ray_shift, ray_weight, band_rows)
    tile_count = lax.axis_size("tile")
    dir_count = lax.axis_size("dir")
    direction_count = ray_shift.shape[0] * dir_count
    summed = jnp.sum(phases, axis=0)
    mean_phase = (
        lax.psum_scatter(
            summed.astype(jnp.bfloat16), "dir", scatter_dimension=1, tiled=True
        ).astype(jnp.float32)
        / direction_count
    )
    tiles_here = influence.shape[1]
    near_count = influence.shape[2]
    block_rows, block_columns = petal.shape
    ext_rows, ext_columns = block_rows + 2, block_columns + 2
    extent = ext_rows * ext_columns
    values = influence.astype(jnp.float32)
    onehot = (influence_index[..., None] == jnp.arange(extent, dtype=jnp.int32)).astype(
        jnp.float32
    )
    weights = pupil_mask.astype(jnp.float32).reshape(band_rows, tiles_here, 128)

    masked = (influence * weights[:, :, None, :].astype(jnp.bfloat16))
    gram = jnp.einsum(
        "rckp,rcjp->rckj", masked, influence, preferred_element_type=jnp.float32
    )
    placed = jnp.einsum("rckj,rcjb->rckb", gram, onehot, precision=highest)
    block_matrix = jnp.einsum("rcka,rckb->ab", onehot, placed, precision=highest)

    field = (weights * mean_phase.reshape(band_rows, tiles_here, 128))
    tile_terms = jnp.einsum("rckp,rcp->rck", values, field, precision=highest)
    block_rhs = jnp.einsum("rck,rcka->a", tile_terms, onehot, precision=highest)

    early = jnp.concatenate([block_matrix.reshape(-1), petal.reshape(-1).astype(jnp.float32)])
    block_count = tile_count * dir_count
    slot = lax.axis_index("tile") * dir_count + lax.axis_index("dir")
    early = lax.psum(
        lax.dynamic_update_slice(
            jnp.zeros((block_count, early.shape[0]), jnp.float32), early[None], (slot, 0)
        ),
        ("tile", "dir"),
    )
    matrices = early[:, : extent * extent].reshape(block_count, extent, extent)
    petal_blocks = early[:, extent * extent :].reshape(
        tile_count, dir_count, block_rows, block_columns
    )
    late = lax.dynamic_update_slice(
        jnp.zeros((block_count, extent), jnp.float32), block_rhs[None], (slot, 0)
    )
    rhs_blocks = lax.psum(late + 0.0 * early[0, 0], ("tile", "dir"))
    grid_rows, grid_columns = tile_count * block_rows, dir_count * block_columns
    petal_grid = petal_blocks.transpose(0, 2, 1, 3).reshape(grid_rows, grid_columns)
    active = (petal_grid < 6).astype(jnp.float32)
    petals = (petal_grid[:, :, None] == jnp.arange(6, dtype=jnp.float32)).astype(jnp.float32)

    def gather_blocks(padded):
        rows = windows(padded, 0, tile_count, block_rows, ext_rows)
        both = windows(rows, 2, dir_count, block_columns, ext_columns)
        return both.transpose(0, 2, 1, 3).reshape(block_count, extent)

    padded_shape = jax.ShapeDtypeStruct((grid_rows + 2, grid_columns + 2), jnp.float32)
    scatter_blocks = jax.linear_transpose(gather_blocks, padded_shape)

    def spread_blocks(blocks):
        (padded,) = scatter_blocks(blocks)
        return padded[1:-1, 1:-1]

    def operator(vector):
        picked = gather_blocks(jnp.pad(vector, 1))
        terms = jnp.einsum("bij,bj->bi", matrices, picked, precision=highest)
        local_part = active * spread_blocks(terms) + ridge_weight * vector
        petal_totals = jnp.einsum("ijp,ij->p", petals, vector, precision=highest)
        return local_part + piston_weight * jnp.einsum(
            "ijp,p->ij", petals, petal_totals, precision=highest
        )

    rhs = active * spread_blocks(rhs_blocks)
    commands = jnp.zeros_like(rhs)
    residual = rhs
    direction = rhs
    norm_now = jnp.sum(residual * residual)
    for step_index in range(ITERS):
        applied = operator(direction)
        step_size = norm_now / jnp.sum(direction * applied)
        commands = commands + step_size * direction
        residual = residual - step_size * applied
        norm_next = jnp.sum(residual * residual)
        direction = residual + (norm_next / norm_now) * direction
        norm_now = norm_next

    row_at = lax.axis_index("tile") * block_rows
    column_at = lax.axis_index("dir") * block_columns
    own = lax.dynamic_slice(commands, (row_at, column_at), (block_rows, block_columns))
    extended = lax.dynamic_slice(
        jnp.pad(commands, 1), (row_at, column_at), (ext_rows, ext_columns)
    )
    picked = jnp.einsum("rcka,a->rck", onehot, extended.reshape(-1), precision=highest)
    fitted = jnp.einsum("rckp,rck->rcp", values, picked, precision=highest).reshape(
        band_rows, tiles_here * 128
    )
    whole_band = lax.all_gather(fitted.astype(jnp.bfloat16), "dir", axis=1, tiled=True).astype(
        fitted.dtype
    )
    corrected = (phases - whole_band[None]).astype(jnp.bfloat16)
    return (own, corrected)


def solution(mesh):
    in_specs = (
        P(None, "tile", None),
        P("dir", None, None),
        P("dir", None, None),
        P("tile", "dir", None),
        P("tile", "dir", None, None),
        P("tile", "dir"),
        P("tile", "dir"),
    )
    out_specs = (P("tile", "dir"), P("dir", "tile", None))
    return jax.shard_map(
        on_device, mesh=mesh, in_specs=in_specs, out_specs=out_specs, check_vma=False
    )
```

profile of v0, /device:TPU:0, one launch (start us, length us, event | category | flops | bytes accessed | tf_op | source)
XLA Modules:
  0.0 442.8 jit_solution(16378414641891634596)
XLA Ops:
  8.0 3.0 collective-permute-start
  11.0 2.6 collective-permute-start.2
  14.8 2.4 fusion.6
  19.5 3.7 fusion.8
  25.5 23.4 %collective-permute-done = bf16[6,64,2048]{2,1,0:T(8,128)(2,1)} collective-permute-done((bf16[6,64,2048]{2,1,0:T(8,128)(2,1)}, bf16[6,64,2048]{2,1,0:T(8,128)(2,1)}, u32[]{:S(2)}, u32[]{:S(2)}) %collective-permute-start) | collective-permute-done | bytes 1572896 | tf_op jit(solution)/shard_map/ppermute | solution.py:22
  50.4 31.1 %collective-permute-done.1 = bf16[6,64,2048]{2,1,0:T(8,128)(2,1)} collective-permute-done((bf16[6,64,2048]{2,1,0:T(8,128)(2,1)}, bf16[6,64,2048]{2,1,0:T(8,128)(2,1)}, u32[]{:S(2)}, u32[]{:S(2)}) %collective-permute-start.1) | collective-permute-done | bytes 1572896 | tf_op jit(solution)/shard_map/ppermute | solution.py:22
  85.0 31.6 %collective-permute-done.3 = bf16[6,64,2048]{2,1,0:T(8,128)(2,1)} collective-permute-done((bf16[6,64,2048]{2,1,0:T(8,128)(2,1)}, bf16[6,64,2048]{2,1,0:T(8,128)(2,1)}, u32[]{:S(2)}, u32[]{:S(2)}) %collective-permute-start.3) | collective-permute-done | bytes 1572896 | tf_op jit(solution)/shard_map/ppermute | solution.py:22
  118.1 3.1 copy-done
  121.2 17.1 %shard_map.86 = f32[4,64,2048]{2,1,0:T(8,128)S(1)} custom-call(s32[4,6,2]{2,1,0:T(8,128)S(1)} %copy.53.shift_ref, f32[4,6,4]{2,1,0:T(8,128)S(1)} %copy.54.gain_ref, bf16[6,320,2048]{2,1,0:T(8,128)(2,1)} %copy-done), custom_call_target="tpu_custom_call" | custom-call | tf_op jit(solution)/shard_map/pallas_call | solution.py:73
  139.2 33.5 %all-reduce.82.cloned.1.call-done = f32[32,4936]{1,0:T(8,128)} async-done(((f32[32,4936]{1,0:T(8,128)}), f32[32,4936]{1,0:T(8,128)}) %all-reduce.82.cloned.1.call-update) | async-done | bytes 631824 | tf_op jit(solution)/shard_map/psum | solution.py:134
  179.4 3.0 fusion.28
  182.5 1.8 fusion.13
  185.5 44.3 %psum.15 = f32[8,5,4,14]{2,0,1,3:T(8,128)} all-reduce(f32[8,5,4,14]{2,0,1,3:T(8,128)} %bitcast.323), channel_id=1, replica_groups=mesh['tile'=8,'dir'=4] {'tile','dir'}, use_global_device_ids=true, to_apply=%region_3.0 | all-reduce | flops 2240 | bytes 17920 | tf_op jit(solution)/shard_map/psum | solution.py:147
  233.2 2.3 pad.246
  235.5 3.5 pad.247
  238.9 2.6 pad.248
  253.7 1.7 copy.60
  257.1 1.7 copy.62
  260.5 1.7 copy.64
  265.6 1.7 copy.67
  271.2 2.2 stack.209
  274.5 1.9 fusion.29
  280.9 2.3 pad.266
  283.2 3.5 pad.267
  286.6 3.5 pad.268
  290.1 2.6 pad.269
  296.5 1.7 fusion.19
  311.1 1.7 copy.76
  317.9 1.7 copy.80
  323.0 1.7 copy.83
  329.3 2.2 stack.230
  332.6 1.9 fusion.30
  338.7 2.3 pad.285
  341.0 3.4 pad.286
  344.4 3.4 pad.287
  347.9 3.5 pad.288
  351.3 2.6 pad.289
  357.9 1.7 fusion.18
  376.6 1.7 copy.90
  380.0 1.7 copy.92
  385.1 1.7 copy.95
  392.1 2.2 stack.251
  395.4 1.9 fusion.31
  402.2 2.3 pad.307
  404.5 2.6 pad.308
  411.2 1.7 fusion.17
  415.3 2.8 fusion.4
  419.2 14.3 %all_gather.3 = bf16[64,2048]{1,0:T(8,128)(2,1)S(1)} all-gather(bf16[64,512]{1,0:T(8,128)(2,1)S(1)} %bitcast.332), channel_id=1, replica_groups=mesh['tile'=8,'dir'=4] {'dir'}, dimensions={1}, use_global_device_ids=true | all-gather | bytes 327680 | tf_op jit(solution)/shard_map/all_gather | solution.py:198
  (273 shorter events, 126.3 us)
Async XLA Ops:
  8.0 164.8 %all-reduce.82.cloned.1.call-start = ((), (), s32[]{:S(2)}) async-start(), calls=%async_computation.1 | async-start | bytes 1277952 | tf_op jit(solution)/shard_map/psum | solution.py:134
  8.0 40.8 %collective-permute-start = (bf16[6,64,2048]{2,1,0:T(8,128)(2,1)}, bf16[6,64,2048]{2,1,0:T(8,128)(2,1)}, u32[]{:S(2)}, u32[]{:S(2)}) collective-permute-start(bf16[6,64,2048]{2,1,0:T(8,128)(2,1)} %param.7), channel_id=1, source_target_pairs={{0,8},{4,12},{8,16},{12,20},{16,24},{20,28},{24,0},{28,4},{1,9},{5... | collective-permute-start | bytes 4718600 | tf_op jit(solution)/shard_map/ppermute | solution.py:22
  11.0 70.6 %collective-permute-start.1 = (bf16[6,64,2048]{2,1,0:T(8,128)(2,1)}, bf16[6,64,2048]{2,1,0:T(8,128)(2,1)}, u32[]{:S(2)}, u32[]{:S(2)}) collective-permute-start(bf16[6,64,2048]{2,1,0:T(8,128)(2,1)} %param.7), channel_id=1, source_target_pairs={{0,4},{4,8},{8,12},{12,16},{16,20},{20,24},{24,28},{28,0},{1,5},{5... | collective-permute-start | bytes 4718600 | tf_op jit(solution)/shard_map/ppermute | solution.py:22
  11.0 72.3 %collective-permute-start.2 = (bf16[6,64,2048]{2,1,0:T(8,128)(2,1)}, bf16[6,64,2048]{2,1,0:T(8,128)(2,1)}, u32[]{:S(2)}, u32[]{:S(2)}) collective-permute-start(bf16[6,64,2048]{2,1,0:T(8,128)(2,1)} %param.7), channel_id=1, source_target_pairs={{0,28},{4,0},{8,4},{12,8},{16,12},{20,16},{24,20},{28,24},{1,29},{... | collective-permute-start | bytes 4718600 | tf_op jit(solution)/shard_map/ppermute | solution.py:22
  13.7 102.9 %collective-permute-start.3 = (bf16[6,64,2048]{2,1,0:T(8,128)(2,1)}, bf16[6,64,2048]{2,1,0:T(8,128)(2,1)}, u32[]{:S(2)}, u32[]{:S(2)}) collective-permute-start(bf16[6,64,2048]{2,1,0:T(8,128)(2,1)} %param.7), channel_id=1, source_target_pairs={{0,24},{4,28},{8,0},{12,4},{16,8},{20,12},{24,16},{28,20},{1,25},{... | collective-permute-start | bytes 4718600 | tf_op jit(solution)/shard_map/ppermute | solution.py:22
  14.7 2.4 copy-start.5
  19.5 3.9 copy-start.9
  19.5 5.7 %copy-start.8 = (s32[4,6,2]{1,2,0:T(2,128)S(1)}, s32[4,6,2]{1,2,0:T(2,128)}, u32[]{:S(2)}) copy-start(s32[4,6,2]{1,2,0:T(2,128)} %param.8) | copy-start | bytes 580
  19.5 5.9 %copy-start.7 = (f32[4,6,4]{1,2,0:T(4,128)S(1)}, f32[4,6,4]{1,2,0:T(4,128)}, u32[]{:S(2)}) copy-start(f32[4,6,4]{1,2,0:T(4,128)} %param.9) | copy-start | bytes 1156
  24.2 0.8 copy-start.2
  25.0 152.8 %reduce-scatter.2.cloned.1.call-start = ((), (), s32[]{:S(2)}) async-start(), calls=%async_computation.2 | async-start | bytes 327680 | tf_op jit(solution)/shard_map/reduce_scatter | solution.py:104
  50.4 32.7 %copy-start.3 = (bf16[6,64,2048]{2,1,0:T(8,128)(2,1)S(1)}, bf16[6,64,2048]{2,1,0:T(8,128)(2,1)}, u32[]{:S(2)}) copy-start(bf16[6,64,2048]{2,1,0:T(8,128)(2,1)} %param.7) | copy-start | bytes 4718596
  118.1 3.1 copy-start
  138.3 39.5 %copy-start.4 = (s32[64,512]{1,0:T(8,128)S(1)}, s32[64,512]{1,0:T(8,128)}, u32[]{:S(2)}) copy-start(s32[64,512]{1,0:T(8,128)} %param.12) | copy-start | bytes 393220
  395.3 19.9 %copy-start.6 = (s32[64,4,16]{0,2,1:T(8,128)S(1)}, s32[64,4,16]{0,2,1:T(8,128)}, u32[]{:S(2)}) copy-start(s32[64,4,16]{0,2,1:T(8,128)} %param.10) | copy-start | bytes 49156
  397.4 20.8 %copy-start.1 = (bf16[64,4,16,128]{3,2,1,0:T(8,128)(2,1)S(1)}, bf16[64,4,16,128]{3,2,1,0:T(8,128)(2,1)}, u32[]{:S(2)}) copy-start(bf16[64,4,16,128]{3,2,1,0:T(8,128)(2,1)} %param.11) | copy-start | bytes 3145732
Sparse Core Ops, SparseCore 0:
  25.1 147.5 all-reduce.81
Sparse Core Ops, SparseCore 1:
  139.3 20.0 reduce-scatter.1
where the time goes:
time: 448 us; the launch traced here: 443 us
  local copies, waits for them, and re-layouts  175 us (39%)
  waiting for transfers between devices  120 us (27%)
  blocking collectives  58.7 us (13%)
  matrix products  30.7 us (7%)
  between operations  23.8 us (5%)
  Pallas kernels  17.1 us (4%)
  other arithmetic  12.1 us (3%)
  starting transfers between devices  6.02 us (1%)
    ppermute x4, waiting for transfers between devices, passed_along(): lax.ppermute(array, axis, [(i, (i + by) % size) for i in range(size)])  86.1 us
    another operation x56, local copies, waits for them, and re-layouts, windows(): return jnp.stack(parts, axis=axis + 1)  71.8 us
    pad x56, local copies, waits for them, and re-layouts, windows(): lax.slice_in_dim(array, offset, offset + stride * (count - 1) + 1, stride...  55.3 us
    psum x1, blocking collectives, on_device(): rhs_blocks = lax.psum(late + 0.0 * early[0, 0], ('tile', 'dir'))  44.3 us
    psum x1, waiting for transfers between devices, on_device(): lax.psum(lax.dynamic_update_slice(jnp.zeros((block_count, early.shape[0])...  33.5 us
    slice x57, local copies, waits for them, and re-layouts, windows(): lax.slice_in_dim(array, offset, offset + stride * (count - 1) + 1, stride...  21.9 us
    pallas_call x1, Pallas kernels, trace_all(): pl.pallas_call(trace_kernel, out_shape=jax.ShapeDtypeStruct((members, ban...  17.1 us
    all_gather x1, blocking collectives, on_device(): lax.all_gather(fitted.astype(jnp.bfloat16), 'dir', axis=1, tiled=True)  14.3 us
  transfers between devices with their start and end apart: 6, of which 4 were waited for; matrix products, arithmetic and copies ran while one was open for 5% of the time, Pallas kernels for 4%

commit v1 on v0

--- a/solution.py
+++ b/solution.py
@@ -92,6 +92,44 @@
     return jnp.stack(parts, axis=axis + 1)
 
 
+def pack_symmetric(matrix):
+    half = matrix.shape[0] // 2
+    first, across, last = matrix[:half, :half], matrix[:half, half:], matrix[half:, half:]
+    row = lax.broadcasted_iota(jnp.int32, (half, half + 1), 0)
+    column = lax.broadcasted_iota(jnp.int32, (half, half + 1), 1)
+    folded = jnp.where(
+        column <= row, jnp.pad(last, ((0, 0), (0, 1))), jnp.pad(first, ((0, 0), (1, 0)))
+    )
+    return jnp.concatenate([folded.reshape(-1), across.reshape(-1)])
+
+
+def unpack_symmetric(packed, extent):
+    half = extent // 2
+    folded = packed[: half * (half + 1)].reshape(half, half + 1)
+    across = packed[half * (half + 1) :].reshape(half, half)
+    row = lax.broadcasted_iota(jnp.int32, (half, half), 0)
+    column = lax.broadcasted_iota(jnp.int32, (half, half), 1)
+    last = jnp.where(column <= row, folded[:, :half], 0.0)
+    first = jnp.where(column >= row, folded[:, 1:], 0.0)
+    diagonal = (row == column).astype(jnp.float32)
+    first = first + first.T * (1.0 - diagonal)
+    last = last + last.T * (1.0 - diagonal)
+    return jnp.concatenate(
+        [jnp.concatenate([first, across], axis=1), jnp.concatenate([across.T, last], axis=1)],
+        axis=0,
+    )
+
+
+def doubling_sum(value, axes):
+    for axis, size in axes:
+        step = 1
+        while step < size:
+            pairs = [(i, i ^ step) for i in range(size)]
+            value = value + lax.ppermute(value, axis, pairs)
+            step *= 2
+    return value
+
+
 def on_device(screens, ray_shift, ray_weight, influence_index, influence, pupil_mask, petal):
     band_rows = screens.shape[1]
     padded_rim = band_stack_whole(screens)
@@ -128,7 +166,7 @@
     tile_terms = jnp.einsum("rckp,rcp->rck", values, field, precision=highest)
     block_rhs = jnp.einsum("rck,rcka->a", tile_terms, onehot, precision=highest)
 
-    early = jnp.concatenate([block_matrix.reshape(-1), petal.reshape(-1).astype(jnp.float32)])
+    early = jnp.concatenate([pack_symmetric(block_matrix), petal.reshape(-1).astype(jnp.float32)])
     block_count = tile_count * dir_count
     slot = lax.axis_index("tile") * dir_count + lax.axis_index("dir")
     early = lax.psum(
@@ -137,41 +175,60 @@
         ),
         ("tile", "dir"),
     )
-    matrices = early[:, : extent * extent].reshape(block_count, extent, extent)
-    petal_blocks = early[:, extent * extent :].reshape(
+    packed_count = extent * extent // 2 + extent // 2
+    matrices = jax.vmap(lambda packed: unpack_symmetric(packed, extent))(early[:, :packed_count])
+    petal_blocks = early[:, packed_count:].reshape(
         tile_count, dir_count, block_rows, block_columns
     )
     late = lax.dynamic_update_slice(
         jnp.zeros((block_count, extent), jnp.float32), block_rhs[None], (slot, 0)
     )
-    rhs_blocks = lax.psum(late + 0.0 * early[0, 0], ("tile", "dir"))
+    rhs_blocks = doubling_sum(late + 0.0 * early[0, 0], (("dir", dir_count), ("tile", tile_count)))
     grid_rows, grid_columns = tile_count * block_rows, dir_count * block_columns
     petal_grid = petal_blocks.transpose(0, 2, 1, 3).reshape(grid_rows, grid_columns)
     active = (petal_grid < 6).astype(jnp.float32)
     petals = (petal_grid[:, :, None] == jnp.arange(6, dtype=jnp.float32)).astype(jnp.float32)
 
+    padded_rows, padded_columns = grid_rows + 2, grid_columns + 2
+    row_pick = (
+        lax.broadcasted_iota(jnp.int32, (tile_count, ext_rows, padded_rows), 2)
+        == block_rows * lax.broadcasted_iota(jnp.int32, (tile_count, ext_rows, padded_rows), 0)
+        + lax.broadcasted_iota(jnp.int32, (tile_count, ext_rows, padded_rows), 1)
+    ).astype(jnp.float32).reshape(tile_count * ext_rows, padded_rows)
+    column_pick = (
+        lax.broadcasted_iota(jnp.int32, (padded_columns, dir_count, ext_columns), 0)
+        == block_columns
+        * lax.broadcasted_iota(jnp.int32, (padded_columns, dir_count, ext_columns), 1)
+        + lax.broadcasted_iota(jnp.int32, (padded_columns, dir_count, ext_columns), 2)
+    ).astype(jnp.float32).reshape(padded_columns, dir_count * ext_columns)
+    block_matrices = matrices.reshape(
+        tile_count, dir_count, ext_rows, ext_columns, ext_rows, ext_columns
+    )
+
     def gather_blocks(padded):
-        rows = windows(padded, 0, tile_count, block_rows, ext_rows)
-        both = windows(rows, 2, dir_count, block_columns, ext_columns)
-        return both.transpose(0, 2, 1, 3).reshape(block_count, extent)
-
-    padded_shape = jax.ShapeDtypeStruct((grid_rows + 2, grid_columns + 2), jnp.float32)
-    scatter_blocks = jax.linear_transpose(gather_blocks, padded_shape)
+        rows = jnp.dot(row_pick, padded, precision=highest)
+        return jnp.dot(rows, column_pick, precision=highest).reshape(
+            tile_count, ext_rows, dir_count, ext_columns
+        )
 
     def spread_blocks(blocks):
-        (padded,) = scatter_blocks(blocks)
+        flat = blocks.reshape(tile_count * ext_rows, dir_count * ext_columns)
+        rows = jnp.dot(row_pick.T, flat, precision=highest)
+        padded = jnp.dot(rows, column_pick.T, precision=highest)
         return padded[1:-1, 1:-1]
 
     def operator(vector):
         picked = gather_blocks(jnp.pad(vector, 1))
-        terms = jnp.einsum("bij,bj->bi", matrices, picked, precision=highest)
+        terms = jnp.einsum("tdklij,tidj->tkdl", block_matrices, picked, precision=highest)
         local_part = active * spread_blocks(terms) + ridge_weight * vector
         petal_totals = jnp.einsum("ijp,ij->p", petals, vector, precision=highest)
         return local_part + piston_weight * jnp.einsum(
             "ijp,p->ij", petals, petal_totals, precision=highest
         )
 
-    rhs = active * spread_blocks(rhs_blocks)
+    rhs = active * spread_blocks(
+        rhs_blocks.reshape(tile_count, dir_count, ext_rows, ext_columns).transpose(0, 2, 1, 3)
+    )
     commands = jnp.zeros_like(rhs)
     residual = rhs
     direction = rhs

time: 448 us -> 268 us (0.60)
  local copies, waits for them, and re-layouts: 175 us -> 38.7 us
  blocking collectives: 58.7 us -> 14.3 us
  waiting for transfers between devices: 120 us -> 102 us
  matrix products: 30.7 us -> 45 us
  starting transfers between devices: 6.02 us -> 12.1 us
    another operation x56 -> x0, local copies, waits for them, and re-layouts: 71.8 us -> none  [windows(): return jnp.stack(parts, axis=axis + 1)]
    pad x59 -> x0, local copies, waits for them, and re-layouts: 55.6 us -> none  [the longest x56 55.3 us: windows(): lax.slice_in_dim(array, offset, offset + stride * (count - 1) + 1, stride...]
    psum x1 -> x0, blocking collectives: 44.3 us -> none  [on_device(): rhs_blocks = lax.psum(late + 0.0 * early[0, 0], ('tile', 'dir'))]
    slice x59 -> x5, local copies, waits for them, and re-layouts: 23.9 us -> 4.01 us  [the longest x1 1.2 us: on_device(): early[0, 0]]
    dot_general x3 -> x17, matrix products: 5.81 us -> 25.3 us  [the longest x3 20.3 us: operator(): jnp.einsum('tdklij,tidj->tkdl', block_matrices, picked, precision=highest)]
    psum x1, waiting for transfers between devices: 33.5 us -> 14.5 us  [on_device(): lax.psum(lax.dynamic_update_slice(jnp.zeros((block_count, early.shape[0])...]
    reshape x14 -> x13, local copies, waits for them, and re-layouts: 6.77 us -> 17.3 us  [the longest x2 15.7 us: on_device(): matrices.reshape(tile_count, dir_count, ext_rows, ext_columns, ext_rows,...]
    ppermute x0 -> x5, starting transfers between devices: none -> 6.09 us  [doubling_sum(): value = value + lax.ppermute(value, axis, pairs)]
  transfers between devices with their start and end apart: 6 -> 11, of which waited for: 4 -> 6; matrix products, arithmetic and copies ran while one was open for 5% -> 19% of each run, Pallas kernels for 4% -> 6%
where the time goes in v1:
time: 268 us; the launch traced here: 267 us
  waiting for transfers between devices  102 us (38%)
  matrix products  45 us (17%)
  local copies, waits for them, and re-layouts  38.7 us (14%)
  between operations  23.4 us (9%)
  Pallas kernels  17.1 us (6%)
  blocking collectives  14.3 us (5%)
  other arithmetic  14.1 us (5%)
  starting transfers between devices  12.1 us (5%)
    ppermute x4, waiting for transfers between devices, passed_along(): lax.ppermute(array, axis, [(i, (i + by) % size) for i in range(size)])  84.4 us
    dot_general x3, matrix products, operator(): jnp.einsum('tdklij,tidj->tkdl', block_matrices, picked, precision=highest)  20.3 us
    pallas_call x1, Pallas kernels, trace_all(): pl.pallas_call(trace_kernel, out_shape=jax.ShapeDtypeStruct((members, ban...  17.1 us
    reshape x2, local copies, waits for them, and re-layouts, on_device(): matrices.reshape(tile_count, dir_count, ext_rows, ext_columns, ext_rows,...  15.7 us
    psum x1, waiting for transfers between devices, on_device(): lax.psum(lax.dynamic_update_slice(jnp.zeros((block_count, early.shape[0])...  14.5 us
    all_gather x1, blocking collectives, on_device(): lax.all_gather(fitted.astype(jnp.bfloat16), 'dir', axis=1, tiled=True)  14.3 us
    unnamed x26, local copies, waits for them, and re-layouts  10.4 us
    ppermute x5, starting transfers between devices, doubling_sum(): value = value + lax.ppermute(value, axis, pairs)  6.09 us
  transfers between devices with their start and end apart: 11, of which 6 were waited for; matrix products, arithmetic and copies ran while one was open for 19% of the time, Pallas kernels for 6%

profile of v1, /device:TPU:0, one launch (start us, length us, event | category | flops | bytes accessed | tf_op | source)
XLA Modules:
  0.0 266.6 jit_solution(1691760112926830944)
XLA Ops:
  8.0 3.0 %collective-permute-start = (bf16[6,64,2048]{2,1,0:T(8,128)(2,1)}, bf16[6,64,2048]{2,1,0:T(8,128)(2,1)}, u32[]{:S(2)}, u32[]{:S(2)}) collective-permute-start(bf16[6,64,2048]{2,1,0:T(8,128)(2,1)} %param.7), channel_id=1, source_target_pairs={{0,8},{4,12},{8,16},{12,20},{16,24},{20,28},{24,0},{28,4},{1,9},{5... | collective-permute-start | bytes 4718600 | tf_op jit(solution)/shard_map/ppermute | solution.py:22
  11.0 2.6 collective-permute-start.2
  13.8 0.9 convert_convert_fusion
  14.7 1.4 iota_compare_fusion
  16.2 2.3 fusion.6
  18.5 1.6 fusion.2
  20.2 3.7 %fusion.8 = f32[70,70]{1,0:T(8,128)S(1)} fusion(f32[64,4,16,70]{3,2,1,0:T(8,128)S(1)} %fusion.2, s32[64,4,16]{0,2,1:T(8,128)S(1)} %copy-done.5), kind=kOutput, calls=%fused_computation.14 | convolution fusion | flops 241131520 | bytes 1182864 | tf_op jit(solution)/shard_map/rcka,rckb->ab/dot_general | solution.py:163
  26.4 21.9 %collective-permute-done = bf16[6,64,2048]{2,1,0:T(8,128)(2,1)} collective-permute-done((bf16[6,64,2048]{2,1,0:T(8,128)(2,1)}, bf16[6,64,2048]{2,1,0:T(8,128)(2,1)}, u32[]{:S(2)}, u32[]{:S(2)}) %collective-permute-start) | collective-permute-done | bytes 1572896 | tf_op jit(solution)/shard_map/ppermute | solution.py:22
  48.3 1.6 constant_dynamic-update-slice_fusion.4
  49.9 31.0 %collective-permute-done.1 = bf16[6,64,2048]{2,1,0:T(8,128)(2,1)} collective-permute-done((bf16[6,64,2048]{2,1,0:T(8,128)(2,1)}, bf16[6,64,2048]{2,1,0:T(8,128)(2,1)}, u32[]{:S(2)}, u32[]{:S(2)}) %collective-permute-start.1) | collective-permute-done | bytes 1572896 | tf_op jit(solution)/shard_map/ppermute | solution.py:22
  80.9 1.6 constant_dynamic-update-slice_fusion.3
  82.7 1.6 constant_dynamic-update-slice_fusion.1
  84.3 31.6 %collective-permute-done.3 = bf16[6,64,2048]{2,1,0:T(8,128)(2,1)} collective-permute-done((bf16[6,64,2048]{2,1,0:T(8,128)(2,1)}, bf16[6,64,2048]{2,1,0:T(8,128)(2,1)}, u32[]{:S(2)}, u32[]{:S(2)}) %collective-permute-start.3) | collective-permute-done | bytes 1572896 | tf_op jit(solution)/shard_map/ppermute | solution.py:22
  115.8 1.6 constant_dynamic-update-slice_fusion.rim_ref
  117.4 3.1 %copy-done = bf16[6,320,2048]{2,1,0:T(8,128)(2,1)} copy-done((bf16[6,320,2048]{2,1,0:T(8,128)(2,1)}, bf16[6,320,2048]{2,1,0:T(8,128)(2,1)S(1)}, u32[]{:S(2)}) %copy-start) | copy-done | bytes 7864344
  120.5 17.1 %shard_map.86 = f32[4,64,2048]{2,1,0:T(8,128)S(1)} custom-call(s32[4,6,2]{2,1,0:T(8,128)S(1)} %copy.29.shift_ref, f32[4,6,4]{2,1,0:T(8,128)S(1)} %copy.30.gain_ref, bf16[6,320,2048]{2,1,0:T(8,128)(2,1)} %copy-done), custom_call_target="tpu_custom_call" | custom-call | tf_op jit(solution)/shard_map/pallas_call | solution.py:73
  137.6 0.9 reduce_sum.63
  138.6 14.5 %all-reduce.8.cloned.1.call-done = f32[32,2521]{1,0:T(8,128)} async-done(((f32[32,2521]{1,0:T(8,128)}), f32[32,2521]{1,0:T(8,128)}) %all-reduce.8.cloned.1.call-update) | async-done | bytes 322704 | tf_op jit(solution)/shard_map/psum | solution.py:172
  153.1 0.9 slice.73
  154.3 1.2 slice.72
  156.1 2.3 reduce-scatter.2.cloned.1.call-done
  158.4 0.9 multiply_multiply_fusion
  159.3 3.0 %fusion.81 = f32[64,4,1,16]{3,2,1,0:T(1,128)S(1)} fusion(f32[64,4,128,1]{2,3,1,0:T(1,128)S(1)} %bitcast.140, bf16[64,4,16,128]{3,2,1,0:T(8,128)(2,1)} %param.11), kind=kOutput, calls=%fused_computation.134 | convolution fusion | flops 6291456 | bytes 1196032 | tf_op jit(solution)/shard_map/rckp,rcp->rck/dot_general | solution.py:166
  162.4 1.0 fusion.20
  163.5 1.4 collective-permute-start.4
  164.9 1.1 fusion.79
  166.0 1.4 copy.65
  167.4 1.4 collective-permute-start.5
  168.8 0.9 broadcast_select_fusion
  169.7 2.3 copy.33
  172.0 1.2 copy.36
  173.2 2.5 fusion.25
  176.7 1.6 collective-permute-start.7
  178.3 1.0 slice.75
  180.5 1.6 collective-permute-start.8
  182.1 2.7 %maximum_maximum_fusion = f32[32,70,70]{2,1,0:T(8,128)} fusion(f32[32,35,35]{2,1,0:T(8,128)} %get-tuple-element.12, f32[32,35,35]{2,1,0:T(8,128)S(1)} %bitcast.127, f32[32,35,35]{2,1,0:T(8,128)S(1)} %reshape.269, f32[32,35,35]{2,1,0:T(8,128)} %get-tuple-element.11), kind=kLoop, calls=%fused_computation.10 | loop fusion | flops 470400 | bytes 1254400 | tf_op jit(solution)/shard_map/vmap()/concatenate | solution.py:117
  184.8 5.8 %reshape.309 = f32[8,4,5,14,5,14]{5,4,3,2,1,0:T(8,128)} reshape(f32[32,70,70]{2,1,0:T(8,128)} %maximum_maximum_fusion) | data formatting | bytes 1254400 | tf_op jit(solution)/shard_map/reshape | solution.py:204
  190.6 9.9 %copy.45 = f32[8,4,5,14,5,14]{3,5,4,2,1,0:T(8,128)} copy(f32[8,4,5,14,5,14]{5,4,3,2,1,0:T(8,128)} %reshape.309) | data formatting | bytes 1254400 | tf_op jit(solution)/shard_map/reshape | solution.py:204
  201.6 1.0 fusion.28
  203.1 6.6 %fusion.41 = f32[8,4,1,5,14,1]{4,2,5,3,1,0:T(1,128)S(1)} fusion(f32[8,4,5,14,5,14]{3,5,4,2,1,0:T(8,128)} %copy.45, f32[8,5,4,14,1,1]{3,1,2,0,4,5:T(8,128)S(1)} %convolution_bitcast_fusion.2), kind=kOutput, calls=%fused_computation.62 | convolution fusion | flops 1881600 | bytes 645120 | tf_op jit(solution)/shard_map/tdklij,tidj->tkdl/dot_general | solution.py:222
  214.9 1.0 fusion.27
  216.2 6.6 %fusion.39 = f32[8,4,1,5,14,1]{4,2,5,3,1,0:T(1,128)S(1)} fusion(f32[8,4,5,14,5,14]{3,5,4,2,1,0:T(8,128)} %copy.45, f32[8,5,4,14,1,1]{3,1,2,0,4,5:T(8,128)S(1)} %convolution_bitcast_fusion.1), kind=kOutput, calls=%fused_computation.59 | convolution fusion | flops 1881600 | bytes 645120 | tf_op jit(solution)/shard_map/tdklij,tidj->tkdl/dot_general | solution.py:222
  227.8 7.0 %fusion.37 = f32[8,4,1,5,14,1]{4,2,5,3,1,0:T(1,128)S(1)} fusion(f32[8,4,5,14,5,14]{3,5,4,2,1,0:T(8,128)} %copy.45, f32[8,5,4,14,1,1]{3,1,2,0,4,5:T(8,128)S(1)} %convolution_bitcast_fusion), kind=kOutput, calls=%fused_computation.56 | convolution fusion | flops 1881600 | bytes 645120 | tf_op jit(solution)/shard_map/tdklij,tidj->tkdl/dot_general | solution.py:222
  235.7 1.0 fusion.26
  239.0 2.8 %fusion.4 = f32[1,64,4,16]{1,0,3,2:T(1,128)S(1)} fusion(s32[64,4,16]{0,2,1:T(8,128)S(1)} %copy-done.5, f32[70,1,1,1]{0,1,2,3:T(1,128)S(1)} %reshape.302), kind=kOutput, calls=%fused_computation.6 | convolution fusion | flops 3727360 | bytes 33048 | tf_op jit(solution)/shard_map/rcka,a->rck/dot_general | solution.py:251
  241.9 1.0 fusion.82
  242.9 14.3 %all_gather.3 = bf16[64,2048]{1,0:T(8,128)(2,1)S(1)} all-gather(bf16[64,512]{1,0:T(8,128)(2,1)S(1)} %bitcast.135), channel_id=1, replica_groups=mesh['tile'=8,'dir'=4] {'dir'}, dimensions={1}, use_global_device_ids=true | all-gather | bytes 327680 | tf_op jit(solution)/shard_map/all_gather | solution.py:255
  257.3 1.2 subtract_convert_fusion
  (115 shorter events, 14.7 us)
Async XLA Ops:
  8.0 145.1 %all-reduce.8.cloned.1.call-start = ((), (), s32[]{:S(2)}) async-start(), calls=%async_computation.1 | async-start | bytes 655360 | tf_op jit(solution)/shard_map/psum | solution.py:172
  8.0 40.3 %collective-permute-start = (bf16[6,64,2048]{2,1,0:T(8,128)(2,1)}, bf16[6,64,2048]{2,1,0:T(8,128)(2,1)}, u32[]{:S(2)}, u32[]{:S(2)}) collective-permute-start(bf16[6,64,2048]{2,1,0:T(8,128)(2,1)} %param.7), channel_id=1, source_target_pairs={{0,8},{4,12},{8,16},{12,20},{16,24},{20,28},{24,0},{28,4},{1,9},{5... | collective-permute-start | bytes 4718600 | tf_op jit(solution)/shard_map/ppermute | solution.py:22
  11.0 69.9 %collective-permute-start.1 = (bf16[6,64,2048]{2,1,0:T(8,128)(2,1)}, bf16[6,64,2048]{2,1,0:T(8,128)(2,1)}, u32[]{:S(2)}, u32[]{:S(2)}) collective-permute-start(bf16[6,64,2048]{2,1,0:T(8,128)(2,1)} %param.7), channel_id=1, source_target_pairs={{0,4},{4,8},{8,12},{12,16},{16,20},{20,24},{24,28},{28,0},{1,5},{5... | collective-permute-start | bytes 4718600 | tf_op jit(solution)/shard_map/ppermute | solution.py:22
  11.0 71.6 %collective-permute-start.2 = (bf16[6,64,2048]{2,1,0:T(8,128)(2,1)}, bf16[6,64,2048]{2,1,0:T(8,128)(2,1)}, u32[]{:S(2)}, u32[]{:S(2)}) collective-permute-start(bf16[6,64,2048]{2,1,0:T(8,128)(2,1)} %param.7), channel_id=1, source_target_pairs={{0,28},{4,0},{8,4},{12,8},{16,12},{20,16},{24,20},{28,24},{1,29},{... | collective-permute-start | bytes 4718600 | tf_op jit(solution)/shard_map/ppermute | solution.py:22
  13.7 102.1 %collective-permute-start.3 = (bf16[6,64,2048]{2,1,0:T(8,128)(2,1)}, bf16[6,64,2048]{2,1,0:T(8,128)(2,1)}, u32[]{:S(2)}, u32[]{:S(2)}) collective-permute-start(bf16[6,64,2048]{2,1,0:T(8,128)(2,1)} %param.7), channel_id=1, source_target_pairs={{0,24},{4,28},{8,0},{12,4},{16,8},{20,12},{24,16},{28,20},{1,25},{... | collective-permute-start | bytes 4718600 | tf_op jit(solution)/shard_map/ppermute | solution.py:22
  18.5 1.6 copy-start.5
  20.1 4.2 %copy-start.8 = (s32[3,12]{1,0:T(4,128)S(1)}, s32[3,12]{1,0:T(4,128)}, u32[]{:S(2)}) copy-start(s32[3,12]{1,0:T(4,128)} %param.13) | copy-start | bytes 436
  20.1 5.6 %copy-start.7 = (s32[4,6,2]{1,2,0:T(2,128)S(1)}, s32[4,6,2]{1,2,0:T(2,128)}, u32[]{:S(2)}) copy-start(s32[4,6,2]{1,2,0:T(2,128)} %param.8) | copy-start | bytes 580
  20.2 5.7 %copy-start.6 = (f32[4,6,4]{1,2,0:T(4,128)S(1)}, f32[4,6,4]{1,2,0:T(4,128)}, u32[]{:S(2)}) copy-start(f32[4,6,4]{1,2,0:T(4,128)} %param.9) | copy-start | bytes 1156
  24.8 0.7 copy-start.3
  25.5 132.9 %reduce-scatter.2.cloned.1.call-start = ((), (), s32[]{:S(2)}) async-start(), calls=%async_computation.2 | async-start | bytes 327680 | tf_op jit(solution)/shard_map/reduce_scatter | solution.py:142
  49.9 32.6 %copy-start.2 = (bf16[6,64,2048]{2,1,0:T(8,128)(2,1)S(1)}, bf16[6,64,2048]{2,1,0:T(8,128)(2,1)}, u32[]{:S(2)}) copy-start(bf16[6,64,2048]{2,1,0:T(8,128)(2,1)} %param.7) | copy-start | bytes 4718596
  117.4 3.1 %copy-start = (bf16[6,320,2048]{2,1,0:T(8,128)(2,1)}, bf16[6,320,2048]{2,1,0:T(8,128)(2,1)S(1)}, u32[]{:S(2)}) copy-start(bf16[6,320,2048]{2,1,0:T(8,128)(2,1)S(1)} %constant_dynamic-update-slice_fusion.rim_ref) | copy-start | bytes 23592964
  137.6 20.9 %copy-start.4 = (s32[64,512]{1,0:T(8,128)S(1)}, s32[64,512]{1,0:T(8,128)}, u32[]{:S(2)}) copy-start(s32[64,512]{1,0:T(8,128)} %param.12) | copy-start | bytes 393220
  163.5 3.9 %collective-permute-start.4 = (f32[32,70]{1,0:T(8,128)S(1)}, f32[32,70]{1,0:T(8,128)S(1)}, u32[]{:S(2)}, u32[]{:S(2)}) collective-permute-start(f32[32,70]{1,0:T(8,128)S(1)} %add.165), channel_id=1, source_target_pairs={{0,1},{1,0},{2,3},{3,2},{4,5},{5,4},{6,7},{7,6},{8,9},{9,8},{10,11... | collective-permute-start | bytes 26888 | tf_op jit(solution)/shard_map/ppermute | solution.py:128
  167.4 5.7 %collective-permute-start.5 = (f32[32,70]{1,0:T(8,128)S(1)}, f32[32,70]{1,0:T(8,128)S(1)}, u32[]{:S(2)}, u32[]{:S(2)}) collective-permute-start(f32[32,70]{1,0:T(8,128)S(1)} %add.166), channel_id=1, source_target_pairs={{0,2},{1,3},{2,0},{3,1},{4,6},{5,7},{6,4},{7,5},{8,10},{9,11},{10,... | collective-permute-start | bytes 26888 | tf_op jit(solution)/shard_map/ppermute | solution.py:128
  173.2 3.6 %collective-permute-start.6 = (f32[32,70]{1,0:T(8,128)S(1)}, f32[32,70]{1,0:T(8,128)S(1)}, u32[]{:S(2)}, u32[]{:S(2)}) collective-permute-start(f32[32,70]{1,0:T(8,128)S(1)} %add.167), channel_id=1, source_target_pairs={{0,4},{4,0},{8,12},{12,8},{16,20},{20,16},{24,28},{28,24},{1,5},{5... | collective-permute-start | bytes 26888 | tf_op jit(solution)/shard_map/ppermute | solution.py:128
  176.7 3.8 %collective-permute-start.7 = (f32[32,70]{1,0:T(8,128)S(1)}, f32[32,70]{1,0:T(8,128)S(1)}, u32[]{:S(2)}, u32[]{:S(2)}) collective-permute-start(f32[32,70]{1,0:T(8,128)S(1)} %add.168), channel_id=1, source_target_pairs={{0,8},{4,12},{8,0},{12,4},{16,24},{20,28},{24,16},{28,20},{1,9},{5... | collective-permute-start | bytes 26888 | tf_op jit(solution)/shard_map/ppermute | solution.py:128
  180.5 20.0 %collective-permute-start.8 = (f32[32,70]{1,0:T(8,128)S(1)}, f32[32,70]{1,0:T(8,128)S(1)}, u32[]{:S(2)}, u32[]{:S(2)}) collective-permute-start(f32[32,70]{1,0:T(8,128)S(1)} %add.169), channel_id=1, source_target_pairs={{0,16},{4,20},{8,24},{12,28},{16,0},{20,4},{24,8},{28,12},{1,17},{... | collective-permute-start | bytes 26888 | tf_op jit(solution)/shard_map/ppermute | solution.py:128
  227.8 14.1 %copy-start.1 = (bf16[64,4,16,128]{3,2,1,0:T(8,128)(2,1)S(1)}, bf16[64,4,16,128]{3,2,1,0:T(8,128)(2,1)}, u32[]{:S(2)}) copy-start(bf16[64,4,16,128]{3,2,1,0:T(8,128)(2,1)} %param.11) | copy-start | bytes 3145732
Sparse Core Ops, SparseCore 0:
  25.7 127.3 all-reduce.7
Sparse Core Ops, SparseCore 1:
  138.5 19.8 reduce-scatter.1

commit v2 on v1

--- a/solution.py
+++ b/solution.py
@@ -120,13 +120,14 @@
     )
 
 
-def doubling_sum(value, axes):
+def slot_gather(value, axes):
     for axis, size in axes:
-        step = 1
-        while step < size:
-            pairs = [(i, i ^ step) for i in range(size)]
-            value = value + lax.ppermute(value, axis, pairs)
-            step *= 2
+        received = [
+            lax.ppermute(value, axis, [(i, (i + offset) % size) for i in range(size)])
+            for offset in range(1, size)
+        ]
+        for part in received:
+            value = value + part
     return value
 
 
@@ -183,7 +184,7 @@
     late = lax.dynamic_update_slice(
         jnp.zeros((block_count, extent), jnp.float32), block_rhs[None], (slot, 0)
     )
-    rhs_blocks = doubling_sum(late + 0.0 * early[0, 0], (("dir", dir_count), ("tile", tile_count)))
+    rhs_blocks = slot_gather(late + 0.0 * early[0, 0], (("dir", dir_count), ("tile", tile_count)))
     grid_rows, grid_columns = tile_count * block_rows, dir_count * block_columns
     petal_grid = petal_blocks.transpose(0, 2, 1, 3).reshape(grid_rows, grid_columns)
     active = (petal_grid < 6).astype(jnp.float32)
@@ -201,34 +202,36 @@
         * lax.broadcasted_iota(jnp.int32, (padded_columns, dir_count, ext_columns), 1)
         + lax.broadcasted_iota(jnp.int32, (padded_columns, dir_count, ext_columns), 2)
     ).astype(jnp.float32).reshape(padded_columns, dir_count * ext_columns)
-    block_matrices = matrices.reshape(
-        tile_count, dir_count, ext_rows, ext_columns, ext_rows, ext_columns
-    )
 
     def gather_blocks(padded):
         rows = jnp.dot(row_pick, padded, precision=highest)
-        return jnp.dot(rows, column_pick, precision=highest).reshape(
-            tile_count, ext_rows, dir_count, ext_columns
+        picked = jnp.dot(rows, column_pick, precision=highest)
+        return (
+            picked.reshape(tile_count, ext_rows, dir_count, ext_columns)
+            .transpose(0, 2, 1, 3)
+            .reshape(block_count, extent)
         )
 
     def spread_blocks(blocks):
-        flat = blocks.reshape(tile_count * ext_rows, dir_count * ext_columns)
+        flat = (
+            blocks.reshape(tile_count, dir_count, ext_rows, ext_columns)
+            .transpose(0, 2, 1, 3)
+            .reshape(tile_count * ext_rows, dir_count * ext_columns)
+        )
         rows = jnp.dot(row_pick.T, flat, precision=highest)
         padded = jnp.dot(rows, column_pick.T, precision=highest)
         return padded[1:-1, 1:-1]
 
     def operator(vector):
         picked = gather_blocks(jnp.pad(vector, 1))
-        terms = jnp.einsum("tdklij,tidj->tkdl", block_matrices, picked, precision=highest)
+        terms = jnp.einsum("bij,bj->bi", matrices, picked, precision=highest)
         local_part = active * spread_blocks(terms) + ridge_weight * vector
         petal_totals = jnp.einsum("ijp,ij->p", petals, vector, precision=highest)
         return local_part + piston_weight * jnp.einsum(
             "ijp,p->ij", petals, petal_totals, precision=highest
         )
 
-    rhs = active * spread_blocks(
-        rhs_blocks.reshape(tile_count, dir_count, ext_rows, ext_columns).transpose(0, 2, 1, 3)
-    )
+    rhs = active * spread_blocks(rhs_blocks)
     commands = jnp.zeros_like(rhs)
     residual = rhs
     direction = rhs

time: 268 us -> 294 us (1.097)
  waiting for transfers between devices: 102 us -> 138 us
  local copies, waits for them, and re-layouts: 38.7 us -> 27.6 us
  matrix products: 45 us -> 42 us
    psum x1, waiting for transfers between devices: 14.5 us -> 125 us  [on_device(): lax.psum(lax.dynamic_update_slice(jnp.zeros((block_count, early.shape[0])...]
    ppermute x4, waiting for transfers between devices: 84.4 us -> 0.01 us  [passed_along(): lax.ppermute(array, axis, [(i, (i + by) % size) for i in range(size)])]
    reshape x7 -> x11, local copies, waits for them, and re-layouts: 16.2 us -> 1.01 us  [the longest x4 0.4 us: spread_blocks(): flat = blocks.reshape(tile_count, dir_count, ext_rows, ext_columns).trans...]
    dot_general x6, matrix products: 21.1 us -> 6.57 us  [the longest x3 5.81 us: operator(): terms = jnp.einsum('bij,bj->bi', matrices, picked, precision=highest)]
    reduce_scatter x1, waiting for transfers between devices: 2.31 us -> 11.5 us  [on_device(): lax.psum_scatter(summed.astype(jnp.bfloat16), 'dir', scatter_dimension=1,...]
    ppermute x5 -> x10, starting transfers between devices: 6.09 us -> 8.47 us  [slot_gather(): lax.ppermute(value, axis, [(i, (i + offset) % size) for i in range(size)])]
    unnamed x26 -> x34, local copies, waits for them, and re-layouts: 10.4 us -> 10.6 us
  transfers between devices with their start and end apart: 11 -> 16, of which waited for: 6 -> 5; matrix products, arithmetic and copies ran while one was open for 19% -> 12% of each run, Pallas kernels for 6% -> 0%
where the time goes in v2:
time: 294 us; the launch traced here: 293 us
  waiting for transfers between devices  138 us (47%)
  matrix products  42 us (14%)
  local copies, waits for them, and re-layouts  27.6 us (9%)
  between operations  23.5 us (8%)
  Pallas kernels  17.1 us (6%)
  other arithmetic  16.1 us (5%)
  starting transfers between devices  14.5 us (5%)
  blocking collectives  14 us (5%)
    psum x1, waiting for transfers between devices, on_device(): lax.psum(lax.dynamic_update_slice(jnp.zeros((block_count, early.shape[0])...  125 us
    pallas_call x1, Pallas kernels, trace_all(): pl.pallas_call(trace_kernel, out_shape=jax.ShapeDtypeStruct((members, ban...  17.1 us
    all_gather x1, blocking collectives, on_device(): lax.all_gather(fitted.astype(jnp.bfloat16), 'dir', axis=1, tiled=True)  14 us
    reduce_scatter x1, waiting for transfers between devices, on_device(): lax.psum_scatter(summed.astype(jnp.bfloat16), 'dir', scatter_dimension=1,...  11.5 us
    unnamed x34, local copies, waits for them, and re-layouts  10.6 us
    ppermute x10, starting transfers between devices, slot_gather(): lax.ppermute(value, axis, [(i, (i + offset) % size) for i in range(size)])  8.47 us
  transfers between devices with their start and end apart: 16, of which 5 were waited for; matrix products, arithmetic and copies ran while one was open for 12% of the time, Pallas kernels for 0%

profile of v2, /device:TPU:0, one launch (start us, length us, event | category | flops | bytes accessed | tf_op | source)
XLA Modules:
  0.0 293.1 jit_solution(15487162095456825506)
XLA Ops:
  8.0 3.0 %collective-permute-start = (bf16[6,64,2048]{2,1,0:T(8,128)(2,1)}, bf16[6,64,2048]{2,1,0:T(8,128)(2,1)}, u32[]{:S(2)}, u32[]{:S(2)}) collective-permute-start(bf16[6,64,2048]{2,1,0:T(8,128)(2,1)} %param.7), channel_id=1, source_target_pairs={{0,8},{4,12},{8,16},{12,20},{16,24},{20,28},{24,0},{28,4},{1,9},{5... | collective-permute-start | bytes 4718600 | tf_op jit(solution)/shard_map/ppermute | solution.py:22
  11.0 2.6 collective-permute-start.2
  14.7 1.4 iota_compare_fusion
  16.2 2.4 fusion.6
  18.6 1.6 fusion.2
  20.3 3.7 %fusion.8 = f32[70,70]{1,0:T(8,128)S(1)} fusion(f32[64,4,16,70]{3,2,1,0:T(8,128)S(1)} %fusion.2, s32[64,4,16]{0,2,1:T(8,128)S(1)} %copy-done.5), kind=kOutput, calls=%fused_computation.14 | convolution fusion | flops 241131520 | bytes 1182864 | tf_op jit(solution)/shard_map/rcka,rckb->ab/dot_general | solution.py:164
  28.4 124.9 %all-reduce.8.cloned.1.call-done = f32[32,2521]{1,0:T(8,128)} async-done(((f32[32,2521]{1,0:T(8,128)}), f32[32,2521]{1,0:T(8,128)}) %all-reduce.8.cloned.1.call-update) | async-done | bytes 322704 | tf_op jit(solution)/shard_map/psum | solution.py:173
  154.5 1.6 constant_dynamic-update-slice_fusion.4
  156.1 1.7 constant_dynamic-update-slice_fusion.3
  158.1 1.6 constant_dynamic-update-slice_fusion.1
  159.7 1.6 constant_dynamic-update-slice_fusion.rim_ref
  161.3 3.0 %copy-done = bf16[6,320,2048]{2,1,0:T(8,128)(2,1)} copy-done((bf16[6,320,2048]{2,1,0:T(8,128)(2,1)}, bf16[6,320,2048]{2,1,0:T(8,128)(2,1)S(1)}, u32[]{:S(2)}) %copy-start) | copy-done | bytes 7864344
  164.3 17.1 %shard_map.86 = f32[4,64,2048]{2,1,0:T(8,128)S(1)} custom-call(s32[4,6,2]{2,1,0:T(8,128)S(1)} %copy.40.shift_ref, f32[4,6,4]{2,1,0:T(8,128)S(1)} %copy.41.gain_ref, bf16[6,320,2048]{2,1,0:T(8,128)(2,1)} %copy-done), custom_call_target="tpu_custom_call" | custom-call | tf_op jit(solution)/shard_map/pallas_call | solution.py:73
  182.3 1.1 fusion.73
  183.4 1.4 copy.87
  184.8 1.6 broadcast_select_fusion
  186.4 2.3 copy.44
  188.7 1.2 copy.47
  189.9 1.2 slice.72
  191.7 11.5 %reduce-scatter.2.cloned.1.call-done = bf16[64,512]{1,0:T(8,128)(2,1)} async-done(((bf16[64,2048]{1,0:T(8,128)(2,1)}), bf16[64,512]{1,0:T(8,128)(2,1)}) %reduce-scatter.2.cloned.1.call-update) | async-done | bytes 65552 | tf_op jit(solution)/shard_map/reduce_scatter | solution.py:143
  203.2 1.5 multiply_multiply_fusion
  204.7 1.6 reshape.296
  206.3 3.0 %fusion.75 = f32[64,4,1,16]{3,2,1,0:T(1,128)S(1)} fusion(f32[64,4,128,1]{2,3,1,0:T(1,128)} %bitcast.134, bf16[64,4,16,128]{3,2,1,0:T(8,128)(2,1)} %param.11), kind=kOutput, calls=%fused_computation.127 | convolution fusion | flops 6291456 | bytes 1196032 | tf_op jit(solution)/shard_map/rckp,rcp->rck/dot_general | solution.py:167
  210.0 1.8 fusion.20
  212.6 1.9 collective-permute-start.4
  214.6 2.5 fusion.25
  218.3 2.3 collective-permute-start.12
  220.5 1.0 slice.75
  221.8 1.2 copy.45
  223.5 1.4 collective-permute-start.10
  225.2 1.3 collective-permute-start.8
  226.5 2.1 maximum_maximum_fusion
  228.6 1.2 collective-permute-done.8
  232.2 1.6 fusion.28
  235.2 1.9 fusion.76
  237.6 1.5 multiply_reduce_fusion.3
  243.3 1.1 convolution_bitcast_fusion.4
  244.4 2.3 fusion.27
  247.2 1.9 fusion.77
  249.6 1.5 multiply_reduce_fusion.1
  255.7 1.9 fusion.78
  258.2 1.1 convolution_bitcast_fusion.3
  259.3 1.7 fusion.26
  261.0 1.4 fusion.29
  263.9 3.5 %fusion.4 = f32[1,64,4,16]{1,0,3,2:T(1,128)S(1)} fusion(s32[64,4,16]{0,2,1:T(8,128)} %param.10, f32[70,1,1,1]{0,1,2,3:T(1,128)S(1)} %reshape.322), kind=kOutput, calls=%fused_computation.6 | convolution fusion | flops 3727360 | bytes 33048 | tf_op jit(solution)/shard_map/rcka,a->rck/dot_general | solution.py:254
  267.5 2.2 fusion.79
  269.8 14.0 %all_gather.3 = bf16[64,2048]{1,0:T(8,128)(2,1)S(1)} all-gather(bf16[64,512]{1,0:T(8,128)(2,1)S(1)} %bitcast.129), channel_id=1, replica_groups=mesh['tile'=8,'dir'=4] {'dir'}, dimensions={1}, use_global_device_ids=true | all-gather | bytes 327680 | tf_op jit(solution)/shard_map/all_gather | solution.py:258
  283.9 1.2 subtract_convert_fusion
  (137 shorter events, 21.4 us)
Async XLA Ops:
  8.0 145.3 %all-reduce.8.cloned.1.call-start = ((), (), s32[]{:S(2)}) async-start(), calls=%async_computation.1 | async-start | bytes 655360 | tf_op jit(solution)/shard_map/psum | solution.py:173
  8.0 146.4 %collective-permute-start = (bf16[6,64,2048]{2,1,0:T(8,128)(2,1)}, bf16[6,64,2048]{2,1,0:T(8,128)(2,1)}, u32[]{:S(2)}, u32[]{:S(2)}) collective-permute-start(bf16[6,64,2048]{2,1,0:T(8,128)(2,1)} %param.7), channel_id=1, source_target_pairs={{0,8},{4,12},{8,16},{12,20},{16,24},{20,28},{24,0},{28,4},{1,9},{5... | collective-permute-start | bytes 4718600 | tf_op jit(solution)/shard_map/ppermute | solution.py:22
  11.0 145.0 %collective-permute-start.1 = (bf16[6,64,2048]{2,1,0:T(8,128)(2,1)}, bf16[6,64,2048]{2,1,0:T(8,128)(2,1)}, u32[]{:S(2)}, u32[]{:S(2)}) collective-permute-start(bf16[6,64,2048]{2,1,0:T(8,128)(2,1)} %param.7), channel_id=1, source_target_pairs={{0,4},{4,8},{8,12},{12,16},{16,20},{20,24},{24,28},{28,0},{1,5},{5... | collective-permute-start | bytes 4718600 | tf_op jit(solution)/shard_map/ppermute | solution.py:22
  11.0 147.1 %collective-permute-start.2 = (bf16[6,64,2048]{2,1,0:T(8,128)(2,1)}, bf16[6,64,2048]{2,1,0:T(8,128)(2,1)}, u32[]{:S(2)}, u32[]{:S(2)}) collective-permute-start(bf16[6,64,2048]{2,1,0:T(8,128)(2,1)} %param.7), channel_id=1, source_target_pairs={{0,28},{4,0},{8,4},{12,8},{16,12},{20,16},{24,20},{28,24},{1,29},{... | collective-permute-start | bytes 4718600 | tf_op jit(solution)/shard_map/ppermute | solution.py:22
  13.7 146.0 %collective-permute-start.3 = (bf16[6,64,2048]{2,1,0:T(8,128)(2,1)}, bf16[6,64,2048]{2,1,0:T(8,128)(2,1)}, u32[]{:S(2)}, u32[]{:S(2)}) collective-permute-start(bf16[6,64,2048]{2,1,0:T(8,128)(2,1)} %param.7), channel_id=1, source_target_pairs={{0,24},{4,28},{8,0},{12,4},{16,8},{20,12},{24,16},{28,20},{1,25},{... | collective-permute-start | bytes 4718600 | tf_op jit(solution)/shard_map/ppermute | solution.py:22
  18.6 1.6 copy-start.5
  20.2 4.2 %copy-start.12 = (s32[3,12]{1,0:T(4,128)S(1)}, s32[3,12]{1,0:T(4,128)}, u32[]{:S(2)}) copy-start(s32[3,12]{1,0:T(4,128)} %param.13) | copy-start | bytes 436
  20.2 7.3 %copy-start.11 = (s32[4,6,2]{1,2,0:T(2,128)S(1)}, s32[4,6,2]{1,2,0:T(2,128)}, u32[]{:S(2)}) copy-start(s32[4,6,2]{1,2,0:T(2,128)} %param.8) | copy-start | bytes 580
  20.3 7.4 %copy-start.10 = (f32[4,6,4]{1,2,0:T(4,128)S(1)}, f32[4,6,4]{1,2,0:T(4,128)}, u32[]{:S(2)}) copy-start(f32[4,6,4]{1,2,0:T(4,128)} %param.9) | copy-start | bytes 1156
  24.9 0.7 copy-start.3
  25.6 177.5 %reduce-scatter.2.cloned.1.call-start = ((), (), s32[]{:S(2)}) async-start(), calls=%async_computation.2 | async-start | bytes 327680 | tf_op jit(solution)/shard_map/reduce_scatter | solution.py:143
  26.0 0.8 copy-start.9
  156.0 1.9 copy-start.2
  161.3 3.1 %copy-start = (bf16[6,320,2048]{2,1,0:T(8,128)(2,1)}, bf16[6,320,2048]{2,1,0:T(8,128)(2,1)S(1)}, u32[]{:S(2)}) copy-start(bf16[6,320,2048]{2,1,0:T(8,128)(2,1)S(1)} %constant_dynamic-update-slice_fusion.rim_ref) | copy-start | bytes 23592964
  184.8 18.3 %copy-start.4 = (s32[64,512]{1,0:T(8,128)S(1)}, s32[64,512]{1,0:T(8,128)}, u32[]{:S(2)}) copy-start(s32[64,512]{1,0:T(8,128)} %param.12) | copy-start | bytes 393220
  211.9 6.2 %collective-permute-start.6 = (f32[32,70]{1,0:T(8,128)S(1)}, f32[32,70]{1,0:T(8,128)S(1)}, u32[]{:S(2)}, u32[]{:S(2)}) collective-permute-start(f32[32,70]{1,0:T(8,128)S(1)} %add.180), channel_id=1, source_target_pairs={{0,3},{1,0},{2,1},{3,2},{4,7},{5,4},{6,5},{7,6},{8,11},{9,8},{10,9... | collective-permute-start | bytes 26888 | tf_op jit(solution)/shard_map/ppermute | solution.py:126
  212.3 5.8 %collective-permute-start.5 = (f32[32,70]{1,0:T(8,128)S(1)}, f32[32,70]{1,0:T(8,128)S(1)}, u32[]{:S(2)}, u32[]{:S(2)}) collective-permute-start(f32[32,70]{1,0:T(8,128)S(1)} %add.180), channel_id=1, source_target_pairs={{0,2},{1,3},{2,0},{3,1},{4,6},{5,7},{6,4},{7,5},{8,10},{9,11},{10,... | collective-permute-start | bytes 26888 | tf_op jit(solution)/shard_map/ppermute | solution.py:126
  212.6 5.6 %collective-permute-start.4 = (f32[32,70]{1,0:T(8,128)S(1)}, f32[32,70]{1,0:T(8,128)S(1)}, u32[]{:S(2)}, u32[]{:S(2)}) collective-permute-start(f32[32,70]{1,0:T(8,128)S(1)} %add.180), channel_id=1, source_target_pairs={{0,1},{1,2},{2,3},{3,0},{4,5},{5,6},{6,7},{7,4},{8,9},{9,10},{10,1... | collective-permute-start | bytes 26888 | tf_op jit(solution)/shard_map/ppermute | solution.py:126
  218.1 14.1 %copy-start.8 = (f32[24,48]{1,0:T(8,128)}, f32[24,48]{1,0:T(8,128)S(1)}, u32[]{:S(2)}) copy-start(f32[24,48]{1,0:T(8,128)S(1)} %reshape.280) | copy-start | bytes 13828
  218.2 6.9 %collective-permute-start.13 = (f32[32,70]{1,0:T(8,128)S(1)}, f32[32,70]{1,0:T(8,128)S(1)}, u32[]{:S(2)}, u32[]{:S(2)}) collective-permute-start(f32[32,70]{1,0:T(8,128)S(1)} %add_add_fusion.1), channel_id=1, source_target_pairs={{0,28},{4,0},{8,4},{12,8},{16,12},{20,16},{24,20},{28,24},{1,29},{... | collective-permute-start | bytes 26888 | tf_op jit(solution)/shard_map/ppermute | solution.py:126
  218.3 8.2 %collective-permute-start.12 = (f32[32,70]{1,0:T(8,128)S(1)}, f32[32,70]{1,0:T(8,128)S(1)}, u32[]{:S(2)}, u32[]{:S(2)}) collective-permute-start(f32[32,70]{1,0:T(8,128)S(1)} %add_add_fusion.1), channel_id=1, source_target_pairs={{0,24},{4,28},{8,0},{12,4},{16,8},{20,12},{24,16},{28,20},{1,25},{... | collective-permute-start | bytes 26888 | tf_op jit(solution)/shard_map/ppermute | solution.py:126
  220.5 29.1 %copy-start.6 = (pred[24,48]{1,0:T(8,128)(4,1)}, pred[24,48]{1,0:T(8,128)(4,1)S(1)}, u32[]{:S(2)}) copy-start(pred[24,48]{1,0:T(8,128)(4,1)S(1)} %broadcast_compare_fusion) | copy-start | bytes 3460
  221.8 4.7 %copy-start.1 = (f32[32,35,35]{2,1,0:T(8,128)}, f32[32,35,35]{2,1,0:T(8,128)S(1)}, u32[]{:S(2)}) copy-start(f32[32,35,35]{2,1,0:T(8,128)S(1)} %reshape.284) | copy-start | bytes 470404
  223.0 5.6 %collective-permute-start.11 = (f32[32,70]{1,0:T(8,128)S(1)}, f32[32,70]{1,0:T(8,128)S(1)}, u32[]{:S(2)}, u32[]{:S(2)}) collective-permute-start(f32[32,70]{1,0:T(8,128)S(1)} %add_add_fusion.1), channel_id=1, source_target_pairs={{0,20},{4,24},{8,28},{12,0},{16,4},{20,8},{24,12},{28,16},{1,21},{... | collective-permute-start | bytes 26888 | tf_op jit(solution)/shard_map/ppermute | solution.py:126
  223.5 5.2 %collective-permute-start.10 = (f32[32,70]{1,0:T(8,128)S(1)}, f32[32,70]{1,0:T(8,128)S(1)}, u32[]{:S(2)}, u32[]{:S(2)}) collective-permute-start(f32[32,70]{1,0:T(8,128)S(1)} %add_add_fusion.1), channel_id=1, source_target_pairs={{0,16},{4,20},{8,24},{12,28},{16,0},{20,4},{24,8},{28,12},{1,17},{... | collective-permute-start | bytes 26888 | tf_op jit(solution)/shard_map/ppermute | solution.py:126
  224.8 3.8 %collective-permute-start.9 = (f32[32,70]{1,0:T(8,128)S(1)}, f32[32,70]{1,0:T(8,128)S(1)}, u32[]{:S(2)}, u32[]{:S(2)}) collective-permute-start(f32[32,70]{1,0:T(8,128)S(1)} %add_add_fusion.1), channel_id=1, source_target_pairs={{0,12},{4,16},{8,20},{12,24},{16,28},{20,0},{24,4},{28,8},{1,13},{... | collective-permute-start | bytes 26888 | tf_op jit(solution)/shard_map/ppermute | solution.py:126
  225.2 4.6 %collective-permute-start.8 = (f32[32,70]{1,0:T(8,128)S(1)}, f32[32,70]{1,0:T(8,128)S(1)}, u32[]{:S(2)}, u32[]{:S(2)}) collective-permute-start(f32[32,70]{1,0:T(8,128)S(1)} %add_add_fusion.1), channel_id=1, source_target_pairs={{0,8},{4,12},{8,16},{12,20},{16,24},{20,28},{24,0},{28,4},{1,9},{5... | collective-permute-start | bytes 26888 | tf_op jit(solution)/shard_map/ppermute | solution.py:126
  226.5 4.1 %collective-permute-start.7 = (f32[32,70]{1,0:T(8,128)S(1)}, f32[32,70]{1,0:T(8,128)S(1)}, u32[]{:S(2)}, u32[]{:S(2)}) collective-permute-start(f32[32,70]{1,0:T(8,128)S(1)} %add_add_fusion.1), channel_id=1, source_target_pairs={{0,4},{4,8},{8,12},{12,16},{16,20},{20,24},{24,28},{28,0},{1,5},{5... | collective-permute-start | bytes 26888 | tf_op jit(solution)/shard_map/ppermute | solution.py:126
  251.1 9.9 %copy-start.7 = (pred[24,48]{1,0:T(8,128)(4,1)S(1)}, pred[24,48]{1,0:T(8,128)(4,1)}, u32[]{:S(2)}) copy-start(pred[24,48]{1,0:T(8,128)(4,1)} %copy-done.6) | copy-start | bytes 3460
Sparse Core Ops, SparseCore 0:
  25.8 127.4 all-reduce.7
Sparse Core Ops, SparseCore 1:
  182.4 20.7 reduce-scatter.1

commit v3 on v2

--- a/solution.py
+++ b/solution.py
@@ -120,15 +120,18 @@
     )
 
 
-def slot_gather(value, axes):
-    for axis, size in axes:
-        received = [
-            lax.ppermute(value, axis, [(i, (i + offset) % size) for i in range(size)])
-            for offset in range(1, size)
-        ]
-        for part in received:
-            value = value + part
-    return value
+def axis_gather(value, axis, size):
+    parts = [value] + [
+        lax.ppermute(value, axis, [(i, (i + offset) % size) for i in range(size)])
+        for offset in range(1, size)
+    ]
+    order = (lax.axis_index(axis) - jnp.arange(size)) % size
+    return jnp.take(jnp.stack(parts), order, axis=0)
+
+
+def mesh_gather(value, tile_count, dir_count):
+    gathered = axis_gather(axis_gather(value, "dir", dir_count), "tile", tile_count)
+    return gathered.reshape((tile_count * dir_count,) + value.shape)
 
 
 def on_device(screens, ray_shift, ray_weight, influence_index, influence, pupil_mask, petal):
@@ -169,22 +172,13 @@
 
     early = jnp.concatenate([pack_symmetric(block_matrix), petal.reshape(-1).astype(jnp.float32)])
     block_count = tile_count * dir_count
-    slot = lax.axis_index("tile") * dir_count + lax.axis_index("dir")
-    early = lax.psum(
-        lax.dynamic_update_slice(
-            jnp.zeros((block_count, early.shape[0]), jnp.float32), early[None], (slot, 0)
-        ),
-        ("tile", "dir"),
-    )
+    early = mesh_gather(early, tile_count, dir_count)
     packed_count = extent * extent // 2 + extent // 2
     matrices = jax.vmap(lambda packed: unpack_symmetric(packed, extent))(early[:, :packed_count])
     petal_blocks = early[:, packed_count:].reshape(
         tile_count, dir_count, block_rows, block_columns
     )
-    late = lax.dynamic_update_slice(
-        jnp.zeros((block_count, extent), jnp.float32), block_rhs[None], (slot, 0)
-    )
-    rhs_blocks = slot_gather(late + 0.0 * early[0, 0], (("dir", dir_count), ("tile", tile_count)))
+    rhs_blocks = mesh_gather(block_rhs, tile_count, dir_count)
     grid_rows, grid_columns = tile_count * block_rows, dir_count * block_columns
     petal_grid = petal_blocks.transpose(0, 2, 1, 3).reshape(grid_rows, grid_columns)
     active = (petal_grid < 6).astype(jnp.float32)

time: 294 us -> 287 us (0.976)
  starting transfers between devices: 14.5 us -> 26 us
  local copies, waits for them, and re-layouts: 27.6 us -> 23.1 us
  waiting for transfers between devices: 138 us -> 134 us
  matrix products: 42 us -> 38.1 us
  other arithmetic: 16.1 us -> 12.5 us
    psum x1 -> x0, waiting for transfers between devices: 125 us -> none  [on_device(): lax.psum(lax.dynamic_update_slice(jnp.zeros((block_count, early.shape[0])...]
    ppermute x10 -> x20, waiting for transfers between devices: 2.04 us -> 115 us  [axis_gather(): lax.ppermute(value, axis, [(i, (i + offset) % size) for i in range(size)])]
    ppermute x10 -> x20, starting transfers between devices: 8.47 us -> 21.2 us  [axis_gather(): lax.ppermute(value, axis, [(i, (i + offset) % size) for i in range(size)])]
    reduce_scatter x1, waiting for transfers between devices: 11.5 us -> 18.7 us  [on_device(): lax.psum_scatter(summed.astype(jnp.bfloat16), 'dir', scatter_dimension=1,...]
    unnamed x34 -> x52, local copies, waits for them, and re-layouts: 10.6 us -> 10.5 us
  transfers between devices with their start and end apart: 16 -> 25, of which waited for: 5 -> 11; matrix products, arithmetic and copies ran while one was open for 12% -> 7% of each run, Pallas kernels for 0% -> 0%
where the time goes in v3:
time: 287 us; the launch traced here: 286 us
  waiting for transfers between devices  134 us (47%)
  matrix products  38.1 us (13%)
  starting transfers between devices  26 us (9%)
  local copies, waits for them, and re-layouts  23.1 us (8%)
  between operations  21.7 us (8%)
  Pallas kernels  17.1 us (6%)
  blocking collectives  14.2 us (5%)
  other arithmetic  12.5 us (4%)
    ppermute x20, waiting for transfers between devices, axis_gather(): lax.ppermute(value, axis, [(i, (i + offset) % size) for i in range(size)])  115 us
    ppermute x20, starting transfers between devices, axis_gather(): lax.ppermute(value, axis, [(i, (i + offset) % size) for i in range(size)])  21.2 us
    reduce_scatter x1, waiting for transfers between devices, on_device(): lax.psum_scatter(summed.astype(jnp.bfloat16), 'dir', scatter_dimension=1,...  18.7 us
    pallas_call x1, Pallas kernels, trace_all(): pl.pallas_call(trace_kernel, out_shape=jax.ShapeDtypeStruct((members, ban...  17.1 us
    all_gather x1, blocking collectives, on_device(): lax.all_gather(fitted.astype(jnp.bfloat16), 'dir', axis=1, tiled=True)  14.2 us
    unnamed x52, local copies, waits for them, and re-layouts  10.5 us
    dot_general x3, matrix products, operator(): terms = jnp.einsum('bij,bj->bi', matrices, picked, precision=highest)  5.81 us
  transfers between devices with their start and end apart: 25, of which 11 were waited for; matrix products, arithmetic and copies ran while one was open for 7% of the time, Pallas kernels for 0%

profile of v3, /device:TPU:0, one launch (start us, length us, event | category | flops | bytes accessed | tf_op | source)
XLA Modules:
  0.0 286.3 jit_solution(8811871688664038832)
XLA Ops:
  8.2 1.4 iota_compare_fusion
  9.6 2.3 fusion.6
  12.0 1.6 fusion.2
  13.6 3.7 %fusion.8 = f32[70,70]{1,0:T(8,128)S(1)} fusion(f32[64,4,16,70]{3,2,1,0:T(8,128)S(1)} %fusion.2, s32[64,4,16]{0,2,1:T(8,128)S(1)} %copy-done.2), kind=kOutput, calls=%fused_computation.18 | convolution fusion | flops 241131520 | bytes 1182864 | tf_op jit(solution)/shard_map/rcka,rckb->ab/dot_general | solution.py:167
  17.9 5.1 %collective-permute-start.2 = (f32[2521]{0:T(1024)S(1)}, f32[2521]{0:T(1024)S(1)}, u32[]{:S(2)}, u32[]{:S(2)}) collective-permute-start(f32[2521]{0:T(1024)S(1)} %concatenate.15), channel_id=1, source_target_pairs={{0,3},{1,0},{2,1},{3,2},{4,7},{5,4},{6,5},{7,6},{8,11},{9,8},{10,9... | collective-permute-start | bytes 30260 | tf_op jit(solution)/shard_map/ppermute | solution.py:125
  24.0 1.5 collective-permute-start.10
  27.6 2.7 collective-permute-start.12
  31.7 94.9 %collective-permute-done.3 = f32[4,2521]{1,0:T(4,128)S(1)} collective-permute-done((f32[4,2521]{1,0:T(4,128)S(1)}, f32[4,2521]{1,0:T(4,128)S(1)}, u32[]{:S(2)}, u32[]{:S(2)}) %collective-permute-start.3) | collective-permute-done | bytes 40368 | tf_op jit(solution)/shard_map/ppermute | solution.py:125
  127.3 4.3 %collective-permute-done.4 = f32[4,2521]{1,0:T(4,128)S(1)} collective-permute-done((f32[4,2521]{1,0:T(4,128)S(1)}, f32[4,2521]{1,0:T(4,128)S(1)}, u32[]{:S(2)}, u32[]{:S(2)}) %collective-permute-start.4) | collective-permute-done | bytes 40368 | tf_op jit(solution)/shard_map/ppermute | solution.py:125
  131.6 3.4 %collective-permute-done.5 = f32[4,2521]{1,0:T(4,128)S(1)} collective-permute-done((f32[4,2521]{1,0:T(4,128)S(1)}, f32[4,2521]{1,0:T(4,128)S(1)}, u32[]{:S(2)}, u32[]{:S(2)}) %collective-permute-start.5) | collective-permute-done | bytes 40368 | tf_op jit(solution)/shard_map/ppermute | solution.py:125
  135.0 1.6 collective-permute-start.6
  136.5 2.4 collective-permute-done.6
  139.0 3.4 %collective-permute-done.7 = f32[4,2521]{1,0:T(4,128)S(1)} collective-permute-done((f32[4,2521]{1,0:T(4,128)S(1)}, f32[4,2521]{1,0:T(4,128)S(1)}, u32[]{:S(2)}, u32[]{:S(2)}) %collective-permute-start.7) | collective-permute-done | bytes 40368 | tf_op jit(solution)/shard_map/ppermute | solution.py:125
  142.4 1.8 collective-permute-start.8
  144.2 2.2 collective-permute-done.8
  146.6 1.7 collective-permute-done.9
  150.5 1.2 copy.46
  151.7 1.2 copy.49
  153.1 1.2 copy.47
  154.4 1.6 constant_dynamic-update-slice_fusion.12
  156.0 1.6 constant_dynamic-update-slice_fusion.11
  157.6 1.6 constant_dynamic-update-slice_fusion.10
  159.2 1.6 constant_dynamic-update-slice_fusion.9
  160.8 1.6 constant_dynamic-update-slice_fusion.8.rim_ref
  162.4 3.1 %copy-done = bf16[6,320,2048]{2,1,0:T(8,128)(2,1)} copy-done((bf16[6,320,2048]{2,1,0:T(8,128)(2,1)}, bf16[6,320,2048]{2,1,0:T(8,128)(2,1)S(1)}, u32[]{:S(2)}) %copy-start) | copy-done | bytes 7864344
  165.4 17.1 %shard_map.86 = f32[4,64,2048]{2,1,0:T(8,128)S(1)} custom-call(s32[4,6,2]{2,1,0:T(8,128)S(1)} %copy.41.shift_ref, f32[4,6,4]{2,1,0:T(8,128)S(1)} %copy.42.gain_ref, bf16[6,320,2048]{2,1,0:T(8,128)(2,1)} %copy-done), custom_call_target="tpu_custom_call" | custom-call | tf_op jit(solution)/shard_map/pallas_call | solution.py:73
  183.4 2.5 fusion.22
  185.9 18.7 %reduce-scatter.2.cloned.1.call-done = bf16[64,512]{1,0:T(8,128)(2,1)} async-done(((bf16[64,2048]{1,0:T(8,128)(2,1)}), bf16[64,512]{1,0:T(8,128)(2,1)}) %reduce-scatter.2.cloned.1.call-update) | async-done | bytes 65552 | tf_op jit(solution)/shard_map/reduce_scatter | solution.py:146
  205.6 3.0 %fusion.78 = f32[64,4,1,16]{3,2,1,0:T(1,128)S(1)} fusion(f32[64,4,128,1]{2,3,1,0:T(1,128)S(1)} %bitcast.173, bf16[64,4,16,128]{3,2,1,0:T(8,128)(2,1)} %param.11), kind=kOutput, calls=%fused_computation.176 | convolution fusion | flops 6291456 | bytes 1196032 | tf_op jit(solution)/shard_map/rckp,rcp->rck/dot_general | solution.py:170
  210.4 1.9 collective-permute-start.14
  212.4 2.1 maximum_maximum_fusion
  214.6 1.2 collective-permute-done.14
  216.6 1.5 collective-permute-start.18
  218.1 2.4 collective-permute-start.19
  221.1 1.5 collective-permute-start.22
  222.5 2.3 collective-permute-start.23
  225.0 1.2 collective-permute-done.23
  228.1 1.6 fusion.25
  230.4 1.9 fusion.79
  232.8 1.6 multiply_reduce_fusion.3
  239.1 2.3 fusion.24
  241.9 1.9 fusion.80
  244.3 1.6 multiply_reduce_fusion.1
  249.9 1.9 fusion.81
  253.5 1.7 fusion.23
  257.5 3.5 %fusion.4 = f32[1,64,4,16]{1,0,3,2:T(1,128)S(1)} fusion(s32[64,4,16]{0,2,1:T(8,128)} %param.10, f32[70,1,1,1]{0,1,2,3:T(1,128)S(1)} %reshape.505), kind=kOutput, calls=%fused_computation.10 | convolution fusion | flops 3727360 | bytes 33048 | tf_op jit(solution)/shard_map/rcka,a->rck/dot_general | solution.py:248
  261.1 2.2 fusion.82
  263.4 14.2 %all_gather.3 = bf16[64,2048]{1,0:T(8,128)(2,1)S(1)} all-gather(bf16[64,512]{1,0:T(8,128)(2,1)S(1)} %bitcast.168), channel_id=1, replica_groups=mesh['tile'=8,'dir'=4] {'dir'}, dimensions={1}, use_global_device_ids=true | all-gather | bytes 327680 | tf_op jit(solution)/shard_map/all_gather | solution.py:252
  (192 shorter events, 26.2 us)
Async XLA Ops:
  7.2 197.4 %reduce-scatter.2.cloned.1.call-start = ((), (), s32[]{:S(2)}) async-start(), calls=%async_computation.1 | async-start | bytes 327680 | tf_op jit(solution)/shard_map/reduce_scatter | solution.py:146
  12.0 1.6 copy-start.2
  13.6 4.2 %copy-start.12 = (s32[3,12]{1,0:T(4,128)S(1)}, s32[3,12]{1,0:T(4,128)}, u32[]{:S(2)}) copy-start(s32[3,12]{1,0:T(4,128)} %param.13) | copy-start | bytes 436
  13.6 13.7 %copy-start.11 = (s32[4,6,2]{1,2,0:T(2,128)S(1)}, s32[4,6,2]{1,2,0:T(2,128)}, u32[]{:S(2)}) copy-start(s32[4,6,2]{1,2,0:T(2,128)} %param.8) | copy-start | bytes 580
  13.6 13.8 %copy-start.8 = (f32[4,6,4]{1,2,0:T(4,128)S(1)}, f32[4,6,4]{1,2,0:T(4,128)}, u32[]{:S(2)}) copy-start(f32[4,6,4]{1,2,0:T(4,128)} %param.9) | copy-start | bytes 1156
  17.9 9.6 %collective-permute-start.2 = (f32[2521]{0:T(1024)S(1)}, f32[2521]{0:T(1024)S(1)}, u32[]{:S(2)}, u32[]{:S(2)}) collective-permute-start(f32[2521]{0:T(1024)S(1)} %concatenate.15), channel_id=1, source_target_pairs={{0,3},{1,0},{2,1},{3,2},{4,7},{5,4},{6,5},{7,6},{8,11},{9,8},{10,9... | collective-permute-start | bytes 30260 | tf_op jit(solution)/shard_map/ppermute | solution.py:125
  23.0 7.3 %collective-permute-start.1 = (f32[2521]{0:T(1024)S(1)}, f32[2521]{0:T(1024)S(1)}, u32[]{:S(2)}, u32[]{:S(2)}) collective-permute-start(f32[2521]{0:T(1024)S(1)} %concatenate.15), channel_id=1, source_target_pairs={{0,2},{1,3},{2,0},{3,1},{4,6},{5,7},{6,4},{7,5},{8,10},{9,11},{10,... | collective-permute-start | bytes 30260 | tf_op jit(solution)/shard_map/ppermute | solution.py:125
  23.0 7.9 %collective-permute-start = (f32[2521]{0:T(1024)S(1)}, f32[2521]{0:T(1024)S(1)}, u32[]{:S(2)}, u32[]{:S(2)}) collective-permute-start(f32[2521]{0:T(1024)S(1)} %concatenate.15), channel_id=1, source_target_pairs={{0,1},{1,2},{2,3},{3,0},{4,5},{5,6},{6,7},{7,4},{8,9},{9,10},{10,1... | collective-permute-start | bytes 30260 | tf_op jit(solution)/shard_map/ppermute | solution.py:125
  24.0 130.4 %collective-permute-start.10 = (bf16[6,64,2048]{2,1,0:T(8,128)(2,1)}, bf16[6,64,2048]{2,1,0:T(8,128)(2,1)}, u32[]{:S(2)}, u32[]{:S(2)}) collective-permute-start(bf16[6,64,2048]{2,1,0:T(8,128)(2,1)} %param.7), channel_id=1, source_target_pairs={{0,8},{4,12},{8,16},{12,20},{16,24},{20,28},{24,0},{28,4},{1,9},{5... | collective-permute-start | bytes 4718600 | tf_op jit(solution)/shard_map/ppermute | solution.py:22
  25.5 130.5 %collective-permute-start.11 = (bf16[6,64,2048]{2,1,0:T(8,128)(2,1)}, bf16[6,64,2048]{2,1,0:T(8,128)(2,1)}, u32[]{:S(2)}, u32[]{:S(2)}) collective-permute-start(bf16[6,64,2048]{2,1,0:T(8,128)(2,1)} %param.7), channel_id=1, source_target_pairs={{0,4},{4,8},{8,12},{12,16},{16,20},{20,24},{24,28},{28,0},{1,5},{5... | collective-permute-start | bytes 4718600 | tf_op jit(solution)/shard_map/ppermute | solution.py:22
  25.5 124.0 %copy-start.6 = (pred[4]{0:T(512)(128)(4,1)}, pred[4]{0:T(512)(128)(4,1)S(1)}, u32[]{:S(2)}) copy-start(pred[4]{0:T(512)(128)(4,1)S(1)} %compare_and_fusion) | copy-start | bytes 16
  25.6 123.9 %copy-start.9 = (s32[1024]{0:T(1024)}, s32[1024]{0:T(1024)S(1)}, u32[]{:S(2)}) copy-start(s32[1024]{0:T(1024)S(1)} %pad_clamp_fusion.1) | copy-start | bytes 12292
  25.7 123.9 %copy-start.10 = (s32[1024]{0:T(1024)}, s32[1024]{0:T(1024)S(1)}, u32[]{:S(2)}) copy-start(s32[1024]{0:T(1024)S(1)} %pad_clamp_fusion) | copy-start | bytes 12292
  26.0 0.5 copy-start.4
  26.5 0.9 copy-start.13
  27.6 131.6 %collective-permute-start.12 = (bf16[6,64,2048]{2,1,0:T(8,128)(2,1)}, bf16[6,64,2048]{2,1,0:T(8,128)(2,1)}, u32[]{:S(2)}, u32[]{:S(2)}) collective-permute-start(bf16[6,64,2048]{2,1,0:T(8,128)(2,1)} %param.7), channel_id=1, source_target_pairs={{0,28},{4,0},{8,4},{12,8},{16,12},{20,16},{24,20},{28,24},{1,29},{... | collective-permute-start | bytes 4718600 | tf_op jit(solution)/shard_map/ppermute | solution.py:22
  30.3 130.5 %collective-permute-start.13 = (bf16[6,64,2048]{2,1,0:T(8,128)(2,1)}, bf16[6,64,2048]{2,1,0:T(8,128)(2,1)}, u32[]{:S(2)}, u32[]{:S(2)}) collective-permute-start(bf16[6,64,2048]{2,1,0:T(8,128)(2,1)} %param.7), channel_id=1, source_target_pairs={{0,24},{4,28},{8,0},{12,4},{16,8},{20,12},{24,16},{28,20},{1,25},{... | collective-permute-start | bytes 4718600 | tf_op jit(solution)/shard_map/ppermute | solution.py:22
  31.6 95.0 %collective-permute-start.3 = (f32[4,2521]{1,0:T(4,128)S(1)}, f32[4,2521]{1,0:T(4,128)S(1)}, u32[]{:S(2)}, u32[]{:S(2)}) collective-permute-start(f32[4,2521]{1,0:T(4,128)S(1)} %broadcast_select_fusion.2), channel_id=1, source_target_pairs={{0,4},{4,8},{8,12},{12,16},{16,20},{20,24},{24,28},{28,0},{1,5},{5... | collective-permute-start | bytes 121016 | tf_op jit(solution)/shard_map/ppermute | solution.py:125
  126.6 4.9 %collective-permute-start.4 = (f32[4,2521]{1,0:T(4,128)S(1)}, f32[4,2521]{1,0:T(4,128)S(1)}, u32[]{:S(2)}, u32[]{:S(2)}) collective-permute-start(f32[4,2521]{1,0:T(4,128)S(1)} %broadcast_select_fusion.2), channel_id=1, source_target_pairs={{0,8},{4,12},{8,16},{12,20},{16,24},{20,28},{24,0},{28,4},{1,9},{5... | collective-permute-start | bytes 121016 | tf_op jit(solution)/shard_map/ppermute | solution.py:125
  131.5 3.4 %collective-permute-start.5 = (f32[4,2521]{1,0:T(4,128)S(1)}, f32[4,2521]{1,0:T(4,128)S(1)}, u32[]{:S(2)}, u32[]{:S(2)}) collective-permute-start(f32[4,2521]{1,0:T(4,128)S(1)} %broadcast_select_fusion.2), channel_id=1, source_target_pairs={{0,12},{4,16},{8,20},{12,24},{16,28},{20,0},{24,4},{28,8},{1,13},{... | collective-permute-start | bytes 121016 | tf_op jit(solution)/shard_map/ppermute | solution.py:125
  135.0 4.0 %collective-permute-start.6 = (f32[4,2521]{1,0:T(4,128)S(1)}, f32[4,2521]{1,0:T(4,128)S(1)}, u32[]{:S(2)}, u32[]{:S(2)}) collective-permute-start(f32[4,2521]{1,0:T(4,128)S(1)} %broadcast_select_fusion.2), channel_id=1, source_target_pairs={{0,16},{4,20},{8,24},{12,28},{16,0},{20,4},{24,8},{28,12},{1,17},{... | collective-permute-start | bytes 121016 | tf_op jit(solution)/shard_map/ppermute | solution.py:125
  139.0 3.4 %collective-permute-start.7 = (f32[4,2521]{1,0:T(4,128)S(1)}, f32[4,2521]{1,0:T(4,128)S(1)}, u32[]{:S(2)}, u32[]{:S(2)}) collective-permute-start(f32[4,2521]{1,0:T(4,128)S(1)} %broadcast_select_fusion.2), channel_id=1, source_target_pairs={{0,20},{4,24},{8,28},{12,0},{16,4},{20,8},{24,12},{28,16},{1,21},{... | collective-permute-start | bytes 121016 | tf_op jit(solution)/shard_map/ppermute | solution.py:125
  142.4 4.0 %collective-permute-start.8 = (f32[4,2521]{1,0:T(4,128)S(1)}, f32[4,2521]{1,0:T(4,128)S(1)}, u32[]{:S(2)}, u32[]{:S(2)}) collective-permute-start(f32[4,2521]{1,0:T(4,128)S(1)} %broadcast_select_fusion.2), channel_id=1, source_target_pairs={{0,24},{4,28},{8,0},{12,4},{16,8},{20,12},{24,16},{28,20},{1,25},{... | collective-permute-start | bytes 121016 | tf_op jit(solution)/shard_map/ppermute | solution.py:125
  146.4 1.8 collective-permute-start.9
  149.7 78.5 %copy-start.3 = (f32[24,48]{1,0:T(8,128)}, f32[24,48]{1,0:T(8,128)S(1)}, u32[]{:S(2)}) copy-start(f32[24,48]{1,0:T(8,128)S(1)} %reshape.432) | copy-start | bytes 13828
  153.1 2.8 copy-start.1
  162.3 3.1 %copy-start = (bf16[6,320,2048]{2,1,0:T(8,128)(2,1)}, bf16[6,320,2048]{2,1,0:T(8,128)(2,1)S(1)}, u32[]{:S(2)}) copy-start(bf16[6,320,2048]{2,1,0:T(8,128)(2,1)S(1)} %constant_dynamic-update-slice_fusion.8.rim_ref) | copy-start | bytes 23592964
  208.6 7.9 %copy-start.7 = (pred[4]{0:T(512)(128)(4,1)S(1)}, pred[4]{0:T(512)(128)(4,1)}, u32[]{:S(2)}) copy-start(pred[4]{0:T(512)(128)(4,1)} %copy-done.6) | copy-start | bytes 16
  209.7 17.3 %copy-start.14 = (pred[8]{0:T(512)(128)(4,1)S(1)}, pred[8]{0:T(512)(128)(4,1)}, u32[]{:S(2)}) copy-start(pred[8]{0:T(512)(128)(4,1)} %copy-done.13) | copy-start | bytes 28
  209.7 4.8 %collective-permute-start.16 = (f32[70]{0:T(128)S(1)}, f32[70]{0:T(128)S(1)}, u32[]{:S(2)}, u32[]{:S(2)}) collective-permute-start(f32[70]{0:T(128)S(1)} %bitcast.187), channel_id=1, source_target_pairs={{0,3},{1,0},{2,1},{3,2},{4,7},{5,4},{6,5},{7,6},{8,11},{9,8},{10,9... | collective-permute-start | bytes 848 | tf_op jit(solution)/shard_map/ppermute | solution.py:125
  210.1 4.4 %collective-permute-start.15 = (f32[70]{0:T(128)S(1)}, f32[70]{0:T(128)S(1)}, u32[]{:S(2)}, u32[]{:S(2)}) collective-permute-start(f32[70]{0:T(128)S(1)} %bitcast.188), channel_id=1, source_target_pairs={{0,2},{1,3},{2,0},{3,1},{4,6},{5,7},{6,4},{7,5},{8,10},{9,11},{10,... | collective-permute-start | bytes 848 | tf_op jit(solution)/shard_map/ppermute | solution.py:125
  210.4 5.3 %collective-permute-start.14 = (f32[70]{0:T(128)S(1)}, f32[70]{0:T(128)S(1)}, u32[]{:S(2)}, u32[]{:S(2)}) collective-permute-start(f32[70]{0:T(128)S(1)} %bitcast.189), channel_id=1, source_target_pairs={{0,1},{1,2},{2,3},{3,0},{4,5},{5,6},{6,7},{7,4},{8,9},{9,10},{10,1... | collective-permute-start | bytes 848 | tf_op jit(solution)/shard_map/ppermute | solution.py:125
  212.4 15.1 %copy-start.5 = (s32[56]{0:T(128)S(1)}, s32[56]{0:T(128)}, u32[]{:S(2)}) copy-start(s32[56]{0:T(128)} %copy-done.4) | copy-start | bytes 676
  212.4 17.4 %copy-start.15 = (s32[40]{0:T(128)S(1)}, s32[40]{0:T(128)}, u32[]{:S(2)}) copy-start(s32[40]{0:T(128)} %add.211) | copy-start | bytes 484
  216.6 4.5 %collective-permute-start.17 = (f32[4,70]{1,0:T(4,128)S(1)}, f32[4,70]{1,0:T(4,128)S(1)}, u32[]{:S(2)}, u32[]{:S(2)}) collective-permute-start(f32[4,70]{1,0:T(4,128)S(1)} %broadcast_select_fusion.3), channel_id=1, source_target_pairs={{0,4},{4,8},{8,12},{12,16},{16,20},{20,24},{24,28},{28,0},{1,5},{5... | collective-permute-start | bytes 3368 | tf_op jit(solution)/shard_map/ppermute | solution.py:125
  216.6 5.9 %collective-permute-start.18 = (f32[4,70]{1,0:T(4,128)S(1)}, f32[4,70]{1,0:T(4,128)S(1)}, u32[]{:S(2)}, u32[]{:S(2)}) collective-permute-start(f32[4,70]{1,0:T(4,128)S(1)} %broadcast_select_fusion.3), channel_id=1, source_target_pairs={{0,8},{4,12},{8,16},{12,20},{16,24},{20,28},{24,0},{28,4},{1,9},{5... | collective-permute-start | bytes 3368 | tf_op jit(solution)/shard_map/ppermute | solution.py:125
  218.1 6.8 %collective-permute-start.19 = (f32[4,70]{1,0:T(4,128)S(1)}, f32[4,70]{1,0:T(4,128)S(1)}, u32[]{:S(2)}, u32[]{:S(2)}) collective-permute-start(f32[4,70]{1,0:T(4,128)S(1)} %broadcast_select_fusion.3), channel_id=1, source_target_pairs={{0,12},{4,16},{8,20},{12,24},{16,28},{20,0},{24,4},{28,8},{1,13},{... | collective-permute-start | bytes 3368 | tf_op jit(solution)/shard_map/ppermute | solution.py:125
  220.5 4.4 %collective-permute-start.20 = (f32[4,70]{1,0:T(4,128)S(1)}, f32[4,70]{1,0:T(4,128)S(1)}, u32[]{:S(2)}, u32[]{:S(2)}) collective-permute-start(f32[4,70]{1,0:T(4,128)S(1)} %broadcast_select_fusion.3), channel_id=1, source_target_pairs={{0,16},{4,20},{8,24},{12,28},{16,0},{20,4},{24,8},{28,12},{1,17},{... | collective-permute-start | bytes 3368 | tf_op jit(solution)/shard_map/ppermute | solution.py:125
  221.0 3.9 %collective-permute-start.21 = (f32[4,70]{1,0:T(4,128)S(1)}, f32[4,70]{1,0:T(4,128)S(1)}, u32[]{:S(2)}, u32[]{:S(2)}) collective-permute-start(f32[4,70]{1,0:T(4,128)S(1)} %broadcast_select_fusion.3), channel_id=1, source_target_pairs={{0,20},{4,24},{8,28},{12,0},{16,4},{20,8},{24,12},{28,16},{1,21},{... | collective-permute-start | bytes 3368 | tf_op jit(solution)/shard_map/ppermute | solution.py:125
  221.1 3.9 %collective-permute-start.22 = (f32[4,70]{1,0:T(4,128)S(1)}, f32[4,70]{1,0:T(4,128)S(1)}, u32[]{:S(2)}, u32[]{:S(2)}) collective-permute-start(f32[4,70]{1,0:T(4,128)S(1)} %broadcast_select_fusion.3), channel_id=1, source_target_pairs={{0,24},{4,28},{8,0},{12,4},{16,8},{20,12},{24,16},{28,20},{1,25},{... | collective-permute-start | bytes 3368 | tf_op jit(solution)/shard_map/ppermute | solution.py:125
  222.5 3.7 %collective-permute-start.23 = (f32[4,70]{1,0:T(4,128)S(1)}, f32[4,70]{1,0:T(4,128)S(1)}, u32[]{:S(2)}, u32[]{:S(2)}) collective-permute-start(f32[4,70]{1,0:T(4,128)S(1)} %broadcast_select_fusion.3), channel_id=1, source_target_pairs={{0,28},{4,0},{8,4},{12,8},{16,12},{20,16},{24,20},{28,24},{1,29},{... | collective-permute-start | bytes 3368 | tf_op jit(solution)/shard_map/ppermute | solution.py:125
Sparse Core Ops, SparseCore 0:
  183.5 21.0 reduce-scatter.1

commit v4 on v3

--- a/solution.py
+++ b/solution.py
@@ -137,17 +137,22 @@
 def on_device(screens, ray_shift, ray_weight, influence_index, influence, pupil_mask, petal):
     band_rows = screens.shape[1]
     padded_rim = band_stack_whole(screens)
+    arrived = jnp.sum(padded_rim[:, ::band_rows, :1].astype(jnp.float32))
     phases = trace_all(padded_rim, ray_shift, ray_weight, band_rows)
     tile_count = lax.axis_size("tile")
     dir_count = lax.axis_size("dir")
     direction_count = ray_shift.shape[0] * dir_count
     summed = jnp.sum(phases, axis=0)
-    mean_phase = (
-        lax.psum_scatter(
-            summed.astype(jnp.bfloat16), "dir", scatter_dimension=1, tiled=True
-        ).astype(jnp.float32)
-        / direction_count
-    )
+    block_width = summed.shape[1] // dir_count
+    by_block = summed.reshape(band_rows, dir_count, block_width).transpose(1, 0, 2)
+    own_column = lax.axis_index("dir")
+    column_sum = jnp.take(by_block, own_column, axis=0)
+    for offset in range(1, dir_count):
+        outgoing = jnp.take(by_block, (own_column + offset) % dir_count, axis=0)
+        column_sum = column_sum + lax.ppermute(
+            outgoing, "dir", [(i, (i + offset) % dir_count) for i in range(dir_count)]
+        )
+    mean_phase = column_sum / direction_count
     tiles_here = influence.shape[1]
     near_count = influence.shape[2]
     block_rows, block_columns = petal.shape
@@ -172,7 +177,7 @@
 
     early = jnp.concatenate([pack_symmetric(block_matrix), petal.reshape(-1).astype(jnp.float32)])
     block_count = tile_count * dir_count
-    early = mesh_gather(early, tile_count, dir_count)
+    early = mesh_gather(early + 0.0 * arrived, tile_count, dir_count)
     packed_count = extent * extent // 2 + extent // 2
     matrices = jax.vmap(lambda packed: unpack_symmetric(packed, extent))(early[:, :packed_count])
     petal_blocks = early[:, packed_count:].reshape(
@@ -249,8 +254,11 @@
     fitted = jnp.einsum("rckp,rck->rcp", values, picked, precision=highest).reshape(
         band_rows, tiles_here * 128
     )
-    whole_band = lax.all_gather(fitted.astype(jnp.bfloat16), "dir", axis=1, tiled=True).astype(
-        fitted.dtype
+    whole_band = (
+        axis_gather(fitted.astype(jnp.bfloat16), "dir", dir_count)
+        .transpose(1, 0, 2)
+        .reshape(band_rows, dir_count * fitted.shape[1])
+        .astype(fitted.dtype)
     )
     corrected = (phases - whole_band[None]).astype(jnp.bfloat16)
     return (own, corrected)

time: 287 us -> 253 us (0.88)
  waiting for transfers between devices: 134 us -> 92.5 us
  local copies, waits for them, and re-layouts: 23.1 us -> 38.3 us
  blocking collectives: 14.2 us -> 0 us
  between operations: 21.7 us -> 8.83 us
  starting transfers between devices: 26 us -> 35.2 us
  other arithmetic: 12.5 us -> 19.3 us
    ppermute x20 -> x23, waiting for transfers between devices: 115 us -> 15.7 us  [axis_gather(): lax.ppermute(value, axis, [(i, (i + offset) % size) for i in range(size)])]
    ppermute x4, waiting for transfers between devices: 0.01 us -> 76.8 us  [passed_along(): lax.ppermute(array, axis, [(i, (i + by) % size) for i in range(size)])]
    reduce_scatter x1 -> x0, waiting for transfers between devices: 18.7 us -> none  [on_device(): lax.psum_scatter(summed.astype(jnp.bfloat16), 'dir', scatter_dimension=1,...]
    all_gather x1 -> x0, blocking collectives: 14.2 us -> none  [on_device(): lax.all_gather(fitted.astype(jnp.bfloat16), 'dir', axis=1, tiled=True)]
    ppermute x20 -> x23, starting transfers between devices: 21.2 us -> 25.6 us  [axis_gather(): lax.ppermute(value, axis, [(i, (i + offset) % size) for i in range(size)])]
    ppermute x0 -> x3, starting transfers between devices: none -> 3.83 us  [on_device(): lax.ppermute(outgoing, 'dir', [(i, (i + offset) % dir_count) for i in ran...]
    unnamed x52 -> x63, local copies, waits for them, and re-layouts: 10.5 us -> 12.4 us
  transfers between devices with their start and end apart: 25 -> 30, of which waited for: 11 -> 13; matrix products, arithmetic and copies ran while one was open for 7% -> 21% of each run, Pallas kernels for 0% -> 7%
where the time goes in v4:
time: 253 us; the launch traced here: 251 us
  waiting for transfers between devices  92.5 us (37%)
  matrix products  40 us (16%)
  local copies, waits for them, and re-layouts  38.3 us (15%)
  starting transfers between devices  35.2 us (14%)
  other arithmetic  19.3 us (8%)
  Pallas kernels  17.1 us (7%)
  between operations  8.83 us (3%)
    ppermute x4, waiting for transfers between devices, passed_along(): lax.ppermute(array, axis, [(i, (i + by) % size) for i in range(size)])  76.8 us
    ppermute x23, starting transfers between devices, axis_gather(): lax.ppermute(value, axis, [(i, (i + offset) % size) for i in range(size)])  25.6 us
    pallas_call x1, Pallas kernels, trace_all(): pl.pallas_call(trace_kernel, out_shape=jax.ShapeDtypeStruct((members, ban...  17.1 us
    ppermute x23, waiting for transfers between devices, axis_gather(): lax.ppermute(value, axis, [(i, (i + offset) % size) for i in range(size)])  15.7 us
    unnamed x63, local copies, waits for them, and re-layouts  12.4 us
    dot_general x3, matrix products, operator(): terms = jnp.einsum('bij,bj->bi', matrices, picked, precision=highest)  5.81 us
    ppermute x4, starting transfers between devices, passed_along(): lax.ppermute(array, axis, [(i, (i + by) % size) for i in range(size)])  5.76 us
    dot_general x3, matrix products, operator(): jnp.einsum('ijp,p->ij', petals, petal_totals, precision=highest)  5.18 us
  transfers between devices with their start and end apart: 30, of which 13 were waited for; matrix products, arithmetic and copies ran while one was open for 21% of the time, Pallas kernels for 7%

profile of v4, /device:TPU:0, one launch (start us, length us, event | category | flops | bytes accessed | tf_op | source)
XLA Modules:
  0.0 251.3 jit_solution(1381967585858403315)
XLA Ops:
  0.6 3.0 %collective-permute-start = (bf16[6,64,2048]{2,1,0:T(8,128)(2,1)}, bf16[6,64,2048]{2,1,0:T(8,128)(2,1)}, u32[]{:S(2)}, u32[]{:S(2)}) collective-permute-start(bf16[6,64,2048]{2,1,0:T(8,128)(2,1)} %param.9), channel_id=1, source_target_pairs={{0,8},{4,12},{8,16},{12,20},{16,24},{20,28},{24,0},{28,4},{1,9},{5... | collective-permute-start | bytes 4718600 | tf_op jit(solution)/shard_map/ppermute | solution.py:22
  3.6 2.6 %collective-permute-start.2 = (bf16[6,64,2048]{2,1,0:T(8,128)(2,1)}, bf16[6,64,2048]{2,1,0:T(8,128)(2,1)}, u32[]{:S(2)}, u32[]{:S(2)}) collective-permute-start(bf16[6,64,2048]{2,1,0:T(8,128)(2,1)} %param.9), channel_id=1, source_target_pairs={{0,28},{4,0},{8,4},{12,8},{16,12},{20,16},{24,20},{28,24},{1,29},{... | collective-permute-start | bytes 4718600 | tf_op jit(solution)/shard_map/ppermute | solution.py:22
  7.3 1.4 iota_compare_fusion
  8.8 2.2 fusion.6
  11.0 1.6 fusion.2
  12.7 3.7 %fusion.8 = f32[70,70]{1,0:T(8,128)S(1)} fusion(f32[64,4,16,70]{3,2,1,0:T(8,128)S(1)} %fusion.2, s32[64,4,16]{0,2,1:T(8,128)S(1)} %copy-done.3), kind=kOutput, calls=%fused_computation.19 | convolution fusion | flops 241131520 | bytes 1182864 | tf_op jit(solution)/shard_map/rcka,rckb->ab/dot_general | solution.py:172
  20.5 19.6 %collective-permute-done = bf16[6,64,2048]{2,1,0:T(8,128)(2,1)} collective-permute-done((bf16[6,64,2048]{2,1,0:T(8,128)(2,1)}, bf16[6,64,2048]{2,1,0:T(8,128)(2,1)}, u32[]{:S(2)}, u32[]{:S(2)}) %collective-permute-start) | collective-permute-done | bytes 1572896 | tf_op jit(solution)/shard_map/ppermute | solution.py:22
  40.1 2.8 %constant_dynamic-update-slice_fusion.4 = bf16[6,320,2048]{2,1,0:T(8,128)(2,1)} fusion(bf16[6,64,2048]{2,1,0:T(8,128)(2,1)} %collective-permute-done), kind=kLoop, calls=%fused_computation.78 | loop fusion | bytes 3145728
  42.9 29.3 %collective-permute-done.1 = bf16[6,64,2048]{2,1,0:T(8,128)(2,1)} collective-permute-done((bf16[6,64,2048]{2,1,0:T(8,128)(2,1)}, bf16[6,64,2048]{2,1,0:T(8,128)(2,1)}, u32[]{:S(2)}, u32[]{:S(2)}) %collective-permute-start.1) | collective-permute-done | bytes 1572896 | tf_op jit(solution)/shard_map/ppermute | solution.py:22
  72.2 2.8 %constant_dynamic-update-slice_fusion.3 = bf16[6,320,2048]{2,1,0:T(8,128)(2,1)} fusion(bf16[6,320,2048]{2,1,0:T(8,128)(2,1)} %constant_dynamic-update-slice_fusion.4, bf16[6,64,2048]{2,1,0:T(8,128)(2,1)} %collective-permute-done.1), kind=kLoop, calls=%fused_computation.77 | loop fusion | bytes 3145728
  76.3 2.8 %constant_dynamic-update-slice_fusion.1 = bf16[6,320,2048]{2,1,0:T(8,128)(2,1)} fusion(bf16[6,320,2048]{2,1,0:T(8,128)(2,1)} %constant_dynamic-update-slice_fusion.2, bf16[6,64,2048]{2,1,0:T(8,128)(2,1)} %collective-permute-done.2), kind=kLoop, calls=%fused_computation.75 | loop fusion | bytes 3145728
  79.1 27.9 %collective-permute-done.3 = bf16[6,64,2048]{2,1,0:T(8,128)(2,1)} collective-permute-done((bf16[6,64,2048]{2,1,0:T(8,128)(2,1)}, bf16[6,64,2048]{2,1,0:T(8,128)(2,1)}, u32[]{:S(2)}, u32[]{:S(2)}) %collective-permute-start.3) | collective-permute-done | bytes 1572896 | tf_op jit(solution)/shard_map/ppermute | solution.py:22
  106.9 2.8 %constant_dynamic-update-slice_fusion.rim_ref = bf16[6,320,2048]{2,1,0:T(8,128)(2,1)} fusion(bf16[6,320,2048]{2,1,0:T(8,128)(2,1)} %constant_dynamic-update-slice_fusion.1, bf16[6,64,2048]{2,1,0:T(8,128)(2,1)} %collective-permute-done.3), kind=kLoop, calls=%fused_computation.74 | loop fusion | bytes 3145728 | tf_op jit(solution)/shard_map/concatenate | solution.py:32
  112.1 1.6 collective-permute-start.4
  113.8 2.6 %collective-permute-start.5 = (f32[2521]{0:T(1024)S(1)}, f32[2521]{0:T(1024)S(1)}, u32[]{:S(2)}, u32[]{:S(2)}) collective-permute-start(f32[2521]{0:T(1024)S(1)} %broadcast_add_fusion), channel_id=1, source_target_pairs={{0,2},{1,3},{2,0},{3,1},{4,6},{5,7},{6,4},{7,5},{8,10},{9,11},{10,... | collective-permute-start | bytes 30260 | tf_op jit(solution)/shard_map/ppermute | solution.py:125
  117.7 17.1 %shard_map.86 = f32[4,64,2048]{2,1,0:T(8,128)S(1)} custom-call(s32[4,6,2]{2,1,0:T(8,128)S(1)} %copy.44.shift_ref, f32[4,6,4]{2,1,0:T(8,128)S(1)} %copy.45.gain_ref, bf16[6,320,2048]{2,1,0:T(8,128)(2,1)} %constant_dynamic-update-slice_fusion.rim_ref), custom_call_target="tpu_custom_call" | custom-call | tf_op jit(solution)/shard_map/pallas_call | solution.py:73
  139.5 2.8 %collective-permute-start.16 = (f32[64,512]{1,0:T(8,128)}, f32[64,512]{1,0:T(8,128)}, u32[]{:S(2)}, u32[]{:S(2)}) collective-permute-start(f32[64,512]{1,0:T(8,128)} %bitcast.186), channel_id=1, source_target_pairs={{0,3},{1,0},{2,1},{3,2},{4,7},{5,4},{6,5},{7,6},{8,11},{9,8},{10,9... | collective-permute-start | bytes 393224 | tf_op jit(solution)/shard_map/ppermute | solution.py:152
  143.2 1.5 collective-permute-start.8
  144.7 2.7 %collective-permute-done.7 = f32[4,2521]{1,0:T(4,128)S(1)} collective-permute-done((f32[4,2521]{1,0:T(4,128)S(1)}, f32[4,2521]{1,0:T(4,128)S(1)}, u32[]{:S(2)}, u32[]{:S(2)}) %collective-permute-start.7) | collective-permute-done | bytes 40368 | tf_op jit(solution)/shard_map/ppermute | solution.py:125
  148.6 2.2 collective-permute-done.9
  154.6 1.8 collective-permute-done.12
  159.1 1.8 fusion.84
  163.2 2.2 copy.52
  166.6 2.0 reshape.503
  168.6 2.3 copy.53
  170.9 1.5 reshape.498
  172.4 1.5 copy.43
  173.8 1.5 reshape.499
  175.3 2.5 %fusion.22 = (f32[32,35,35]{2,1,0:T(8,128)}, f32[32,35,35]{2,1,0:T(8,128)}) fusion(f32[32,35,35]{2,1,0:T(8,128)} %copy.52, f32[35,35]{1,0:T(8,128)} %convert_subtract_fusion, f32[32,35,35]{2,1,0:T(8,128)S(1)} %get-tuple-element.19, f32[32,35,35]{1,2,0:T(8,128)} %copy.55, f32[32,35,35]{1,2,0:T(8,128)S(1)} %copy.100, pred[35,35]{0,1:T(8,128)(4,1)} %copy-done.7), kind=kLoop, calls=%fused_computation.41 | loop fusion | flops 196000 | bytes 946925 | tf_op jit(solution)/shard_map/vmap()/add | solution.py:115
  179.6 3.0 %fusion.86 = f32[64,4,1,16]{3,2,1,0:T(1,128)S(1)} fusion(f32[64,4,128,1]{2,3,1,0:T(1,128)S(1)} %bitcast.201, bf16[64,4,16,128]{3,2,1,0:T(8,128)(2,1)} %param.13), kind=kOutput, calls=%fused_computation.197 | convolution fusion | flops 6291456 | bytes 1196032 | tf_op jit(solution)/shard_map/rckp,rcp->rck/dot_general | solution.py:175
  185.7 2.8 %collective-permute-start.19 = (f32[70]{0:T(128)S(1)}, f32[70]{0:T(128)S(1)}, u32[]{:S(2)}, u32[]{:S(2)}) collective-permute-start(f32[70]{0:T(128)S(1)} %bitcast.223), channel_id=1, source_target_pairs={{0,3},{1,0},{2,1},{3,2},{4,7},{5,4},{6,5},{7,6},{8,11},{9,8},{10,9... | collective-permute-start | bytes 848 | tf_op jit(solution)/shard_map/ppermute | solution.py:125
  188.5 2.1 maximum_maximum_fusion
  192.1 1.7 collective-permute-start.21
  197.5 2.4 collective-permute-start.26
  203.3 1.9 fusion.87
  206.9 1.7 fusion.25
  208.6 1.5 multiply_reduce_fusion.3
  214.7 1.9 fusion.88
  218.2 1.7 fusion.24
  220.0 1.5 multiply_reduce_fusion.1
  226.7 1.7 fusion.23
  228.9 1.9 fusion.89
  231.3 1.4 fusion.26
  234.3 3.5 %fusion.4 = f32[1,64,4,16]{1,0,3,2:T(1,128)S(1)} fusion(s32[64,4,16]{0,2,1:T(8,128)} %param.12, f32[70,1,1,1]{0,1,2,3:T(1,128)S(1)} %reshape.657), kind=kOutput, calls=%fused_computation.11 | convolution fusion | flops 3727360 | bytes 33048 | tf_op jit(solution)/shard_map/rcka,a->rck/dot_general | solution.py:253
  238.0 2.2 fusion.90
  241.1 2.9 %collective-permute-start.28 = (bf16[64,512]{1,0:T(8,128)(2,1)S(1)}, bf16[64,512]{1,0:T(8,128)(2,1)S(1)}, u32[]{:S(2)}, u32[]{:S(2)}) collective-permute-start(bf16[64,512]{1,0:T(8,128)(2,1)S(1)} %bitcast.213), channel_id=1, source_target_pairs={{0,2},{1,3},{2,0},{3,1},{4,6},{5,7},{6,4},{7,5},{8,10},{9,11},{10,... | collective-permute-start | bytes 196616 | tf_op jit(solution)/shard_map/ppermute | solution.py:125
  244.8 2.3 collective-permute-done.27
  247.1 1.8 collective-permute-done.28
  (226 shorter events, 52.1 us)
Async XLA Ops:
  0.6 39.5 %collective-permute-start = (bf16[6,64,2048]{2,1,0:T(8,128)(2,1)}, bf16[6,64,2048]{2,1,0:T(8,128)(2,1)}, u32[]{:S(2)}, u32[]{:S(2)}) collective-permute-start(bf16[6,64,2048]{2,1,0:T(8,128)(2,1)} %param.9), channel_id=1, source_target_pairs={{0,8},{4,12},{8,16},{12,20},{16,24},{20,28},{24,0},{28,4},{1,9},{5... | collective-permute-start | bytes 4718600 | tf_op jit(solution)/shard_map/ppermute | solution.py:22
  3.6 68.5 %collective-permute-start.1 = (bf16[6,64,2048]{2,1,0:T(8,128)(2,1)}, bf16[6,64,2048]{2,1,0:T(8,128)(2,1)}, u32[]{:S(2)}, u32[]{:S(2)}) collective-permute-start(bf16[6,64,2048]{2,1,0:T(8,128)(2,1)} %param.9), channel_id=1, source_target_pairs={{0,4},{4,8},{8,12},{12,16},{16,20},{20,24},{24,28},{28,0},{1,5},{5... | collective-permute-start | bytes 4718600 | tf_op jit(solution)/shard_map/ppermute | solution.py:22
  3.6 72.7 %collective-permute-start.2 = (bf16[6,64,2048]{2,1,0:T(8,128)(2,1)}, bf16[6,64,2048]{2,1,0:T(8,128)(2,1)}, u32[]{:S(2)}, u32[]{:S(2)}) collective-permute-start(bf16[6,64,2048]{2,1,0:T(8,128)(2,1)} %param.9), channel_id=1, source_target_pairs={{0,28},{4,0},{8,4},{12,8},{16,12},{20,16},{24,20},{28,24},{1,29},{... | collective-permute-start | bytes 4718600 | tf_op jit(solution)/shard_map/ppermute | solution.py:22
  6.3 100.7 %collective-permute-start.3 = (bf16[6,64,2048]{2,1,0:T(8,128)(2,1)}, bf16[6,64,2048]{2,1,0:T(8,128)(2,1)}, u32[]{:S(2)}, u32[]{:S(2)}) collective-permute-start(bf16[6,64,2048]{2,1,0:T(8,128)(2,1)} %param.9), channel_id=1, source_target_pairs={{0,24},{4,28},{8,0},{12,4},{16,8},{20,12},{24,16},{28,20},{1,25},{... | collective-permute-start | bytes 4718600 | tf_op jit(solution)/shard_map/ppermute | solution.py:22
  12.7 4.4 %copy-start.17 = (s32[3,12]{1,0:T(4,128)S(1)}, s32[3,12]{1,0:T(4,128)}, u32[]{:S(2)}) copy-start(s32[3,12]{1,0:T(4,128)} %param.15) | copy-start | bytes 436
  12.7 4.8 %copy-start.16 = (s32[4,6,2]{1,2,0:T(2,128)S(1)}, s32[4,6,2]{1,2,0:T(2,128)}, u32[]{:S(2)}) copy-start(s32[4,6,2]{1,2,0:T(2,128)} %param.10) | copy-start | bytes 580
  12.7 5.1 %copy-start.13 = (f32[4,6,4]{1,2,0:T(4,128)S(1)}, f32[4,6,4]{1,2,0:T(4,128)}, u32[]{:S(2)}) copy-start(f32[4,6,4]{1,2,0:T(4,128)} %param.11) | copy-start | bytes 1156
  18.9 21.3 %copy-start.8 = (s32[56]{0:T(128)}, s32[56]{0:T(128)S(1)}, u32[]{:S(2)}) copy-start(s32[56]{0:T(128)S(1)} %add.271) | copy-start | bytes 676
  19.2 123.9 %copy-start.10 = (pred[4]{0:T(512)(128)(4,1)}, pred[4]{0:T(512)(128)(4,1)S(1)}, u32[]{:S(2)}) copy-start(pred[4]{0:T(512)(128)(4,1)S(1)} %compare_and_fusion) | copy-start | bytes 16
  19.2 123.2 %copy-start.14 = (s32[1024]{0:T(1024)}, s32[1024]{0:T(1024)S(1)}, u32[]{:S(2)}) copy-start(s32[1024]{0:T(1024)S(1)} %pad_clamp_fusion.1) | copy-start | bytes 12292
  19.3 137.1 %copy-start.15 = (s32[1024]{0:T(1024)}, s32[1024]{0:T(1024)S(1)}, u32[]{:S(2)}) copy-start(s32[1024]{0:T(1024)S(1)} %pad_clamp_fusion) | copy-start | bytes 12292
  19.9 142.4 %copy-start.7 = (pred[35,35]{0,1:T(8,128)(4,1)}, pred[35,35]{0,1:T(8,128)(4,1)S(1)}, u32[]{:S(2)}) copy-start(pred[35,35]{0,1:T(8,128)(4,1)S(1)} %iota_compare_fusion.21) | copy-start | bytes 3679
  42.9 32.1 %copy-start = (bf16[6,64,2048]{2,1,0:T(8,128)(2,1)S(1)}, bf16[6,64,2048]{2,1,0:T(8,128)(2,1)}, u32[]{:S(2)}) copy-start(bf16[6,64,2048]{2,1,0:T(8,128)(2,1)} %param.9) | copy-start | bytes 4718596
  112.1 27.4 %collective-permute-start.4 = (f32[2521]{0:T(1024)S(1)}, f32[2521]{0:T(1024)S(1)}, u32[]{:S(2)}, u32[]{:S(2)}) collective-permute-start(f32[2521]{0:T(1024)S(1)} %broadcast_add_fusion), channel_id=1, source_target_pairs={{0,1},{1,2},{2,3},{3,0},{4,5},{5,6},{6,7},{7,4},{8,9},{9,10},{10,1... | collective-permute-start | bytes 30260 | tf_op jit(solution)/shard_map/ppermute | solution.py:125
  113.8 28.6 %collective-permute-start.5 = (f32[2521]{0:T(1024)S(1)}, f32[2521]{0:T(1024)S(1)}, u32[]{:S(2)}, u32[]{:S(2)}) collective-permute-start(f32[2521]{0:T(1024)S(1)} %broadcast_add_fusion), channel_id=1, source_target_pairs={{0,2},{1,3},{2,0},{3,1},{4,6},{5,7},{6,4},{7,5},{8,10},{9,11},{10,... | collective-permute-start | bytes 30260 | tf_op jit(solution)/shard_map/ppermute | solution.py:125
  116.4 26.0 %collective-permute-start.6 = (f32[2521]{0:T(1024)S(1)}, f32[2521]{0:T(1024)S(1)}, u32[]{:S(2)}, u32[]{:S(2)}) collective-permute-start(f32[2521]{0:T(1024)S(1)} %broadcast_add_fusion), channel_id=1, source_target_pairs={{0,3},{1,0},{2,1},{3,2},{4,7},{5,4},{6,5},{7,6},{8,11},{9,8},{10,9... | collective-permute-start | bytes 30260 | tf_op jit(solution)/shard_map/ppermute | solution.py:125
  137.2 41.3 %collective-permute-start.14 = (f32[64,512]{1,0:T(8,128)}, f32[64,512]{1,0:T(8,128)}, u32[]{:S(2)}, u32[]{:S(2)}) collective-permute-start(f32[64,512]{1,0:T(8,128)} %fusion.35), channel_id=1, source_target_pairs={{0,1},{1,2},{2,3},{3,0},{4,5},{5,6},{6,7},{7,4},{8,9},{9,10},{10,1... | collective-permute-start | bytes 393224 | tf_op jit(solution)/shard_map/ppermute | solution.py:152
  138.5 39.9 %collective-permute-start.15 = (f32[64,512]{1,0:T(8,128)}, f32[64,512]{1,0:T(8,128)}, u32[]{:S(2)}, u32[]{:S(2)}) collective-permute-start(f32[64,512]{1,0:T(8,128)} %fusion.34), channel_id=1, source_target_pairs={{0,2},{1,3},{2,0},{3,1},{4,6},{5,7},{6,4},{7,5},{8,10},{9,11},{10,... | collective-permute-start | bytes 393224 | tf_op jit(solution)/shard_map/ppermute | solution.py:152
  139.5 38.9 %collective-permute-start.16 = (f32[64,512]{1,0:T(8,128)}, f32[64,512]{1,0:T(8,128)}, u32[]{:S(2)}, u32[]{:S(2)}) collective-permute-start(f32[64,512]{1,0:T(8,128)} %bitcast.186), channel_id=1, source_target_pairs={{0,3},{1,0},{2,1},{3,2},{4,7},{5,4},{6,5},{7,6},{8,11},{9,8},{10,9... | collective-permute-start | bytes 393224 | tf_op jit(solution)/shard_map/ppermute | solution.py:152
  143.1 4.3 %collective-permute-start.7 = (f32[4,2521]{1,0:T(4,128)S(1)}, f32[4,2521]{1,0:T(4,128)S(1)}, u32[]{:S(2)}, u32[]{:S(2)}) collective-permute-start(f32[4,2521]{1,0:T(4,128)S(1)} %broadcast_select_fusion.3), channel_id=1, source_target_pairs={{0,4},{4,8},{8,12},{12,16},{16,20},{20,24},{24,28},{28,0},{1,5},{5... | collective-permute-start | bytes 121016 | tf_op jit(solution)/shard_map/ppermute | solution.py:125
  143.2 4.9 %collective-permute-start.8 = (f32[4,2521]{1,0:T(4,128)S(1)}, f32[4,2521]{1,0:T(4,128)S(1)}, u32[]{:S(2)}, u32[]{:S(2)}) collective-permute-start(f32[4,2521]{1,0:T(4,128)S(1)} %broadcast_select_fusion.3), channel_id=1, source_target_pairs={{0,8},{4,12},{8,16},{12,20},{16,24},{20,28},{24,0},{28,4},{1,9},{5... | collective-permute-start | bytes 121016 | tf_op jit(solution)/shard_map/ppermute | solution.py:125
  147.5 3.4 %collective-permute-start.9 = (f32[4,2521]{1,0:T(4,128)S(1)}, f32[4,2521]{1,0:T(4,128)S(1)}, u32[]{:S(2)}, u32[]{:S(2)}) collective-permute-start(f32[4,2521]{1,0:T(4,128)S(1)} %broadcast_select_fusion.3), channel_id=1, source_target_pairs={{0,12},{4,16},{8,20},{12,24},{16,28},{20,0},{24,4},{28,8},{1,13},{... | collective-permute-start | bytes 121016 | tf_op jit(solution)/shard_map/ppermute | solution.py:125
  148.1 4.2 %collective-permute-start.10 = (f32[4,2521]{1,0:T(4,128)S(1)}, f32[4,2521]{1,0:T(4,128)S(1)}, u32[]{:S(2)}, u32[]{:S(2)}) collective-permute-start(f32[4,2521]{1,0:T(4,128)S(1)} %broadcast_select_fusion.3), channel_id=1, source_target_pairs={{0,16},{4,20},{8,24},{12,28},{16,0},{20,4},{24,8},{28,12},{1,17},{... | collective-permute-start | bytes 121016 | tf_op jit(solution)/shard_map/ppermute | solution.py:125
  150.9 3.4 %collective-permute-start.11 = (f32[4,2521]{1,0:T(4,128)S(1)}, f32[4,2521]{1,0:T(4,128)S(1)}, u32[]{:S(2)}, u32[]{:S(2)}) collective-permute-start(f32[4,2521]{1,0:T(4,128)S(1)} %broadcast_select_fusion.3), channel_id=1, source_target_pairs={{0,20},{4,24},{8,28},{12,0},{16,4},{20,8},{24,12},{28,16},{1,21},{... | collective-permute-start | bytes 121016 | tf_op jit(solution)/shard_map/ppermute | solution.py:125
  152.4 4.0 %collective-permute-start.12 = (f32[4,2521]{1,0:T(4,128)S(1)}, f32[4,2521]{1,0:T(4,128)S(1)}, u32[]{:S(2)}, u32[]{:S(2)}) collective-permute-start(f32[4,2521]{1,0:T(4,128)S(1)} %broadcast_select_fusion.3), channel_id=1, source_target_pairs={{0,24},{4,28},{8,0},{12,4},{16,8},{20,12},{24,16},{28,20},{1,25},{... | collective-permute-start | bytes 121016 | tf_op jit(solution)/shard_map/ppermute | solution.py:125
  154.3 2.1 collective-permute-start.13
  170.9 7.6 %copy-start.1 = (s32[64,512]{1,0:T(8,128)S(1)}, s32[64,512]{1,0:T(8,128)}, u32[]{:S(2)}) copy-start(s32[64,512]{1,0:T(8,128)} %param.14) | copy-start | bytes 393220
  175.3 3.1 %copy-start.2 = (f32[1,64,512]{2,0,1:T(1,128)S(1)}, f32[1,64,512]{2,0,1:T(1,128)}, u32[]{:S(2)}) copy-start(f32[1,64,512]{2,0,1:T(1,128)} %get-tuple-element.20) | copy-start | bytes 393220
  177.8 4.8 %copy-start.4 = (s32[64,4,16]{0,2,1:T(8,128)S(1)}, s32[64,4,16]{0,2,1:T(8,128)}, u32[]{:S(2)}) copy-start(s32[64,4,16]{0,2,1:T(8,128)} %param.12) | copy-start | bytes 49156
  182.7 8.7 %copy-start.11 = (pred[4]{0:T(512)(128)(4,1)S(1)}, pred[4]{0:T(512)(128)(4,1)}, u32[]{:S(2)}) copy-start(pred[4]{0:T(512)(128)(4,1)} %copy-done.10) | copy-start | bytes 16
  183.7 18.2 %copy-start.19 = (pred[8]{0:T(512)(128)(4,1)S(1)}, pred[8]{0:T(512)(128)(4,1)}, u32[]{:S(2)}) copy-start(pred[8]{0:T(512)(128)(4,1)} %copy-done.18) | copy-start | bytes 28
  183.7 6.9 %collective-permute-start.17 = (f32[70]{0:T(128)S(1)}, f32[70]{0:T(128)S(1)}, u32[]{:S(2)}, u32[]{:S(2)}) collective-permute-start(f32[70]{0:T(128)S(1)} %bitcast.221), channel_id=1, source_target_pairs={{0,1},{1,2},{2,3},{3,0},{4,5},{5,6},{6,7},{7,4},{8,9},{9,10},{10,1... | collective-permute-start | bytes 848 | tf_op jit(solution)/shard_map/ppermute | solution.py:125
  184.2 6.4 %collective-permute-start.18 = (f32[70]{0:T(128)S(1)}, f32[70]{0:T(128)S(1)}, u32[]{:S(2)}, u32[]{:S(2)}) collective-permute-start(f32[70]{0:T(128)S(1)} %bitcast.222), channel_id=1, source_target_pairs={{0,2},{1,3},{2,0},{3,1},{4,6},{5,7},{6,4},{7,5},{8,10},{9,11},{10,... | collective-permute-start | bytes 848 | tf_op jit(solution)/shard_map/ppermute | solution.py:125
  185.7 5.0 %collective-permute-start.19 = (f32[70]{0:T(128)S(1)}, f32[70]{0:T(128)S(1)}, u32[]{:S(2)}, u32[]{:S(2)}) collective-permute-start(f32[70]{0:T(128)S(1)} %bitcast.223), channel_id=1, source_target_pairs={{0,3},{1,0},{2,1},{3,2},{4,7},{5,4},{6,5},{7,6},{8,11},{9,8},{10,9... | collective-permute-start | bytes 848 | tf_op jit(solution)/shard_map/ppermute | solution.py:125
  188.5 13.9 %copy-start.5 = (pred[24,48]{1,0:T(8,128)(4,1)S(1)}, pred[24,48]{1,0:T(8,128)(4,1)}, u32[]{:S(2)}) copy-start(pred[24,48]{1,0:T(8,128)(4,1)} %broadcast_compare_fusion) | copy-start | bytes 3460
  188.5 13.9 %copy-start.9 = (s32[56]{0:T(128)S(1)}, s32[56]{0:T(128)}, u32[]{:S(2)}) copy-start(s32[56]{0:T(128)} %copy-done.8) | copy-start | bytes 676
  188.5 14.1 %copy-start.20 = (s32[40]{0:T(128)S(1)}, s32[40]{0:T(128)}, u32[]{:S(2)}) copy-start(s32[40]{0:T(128)} %add.274) | copy-start | bytes 484
  191.4 4.6 %collective-permute-start.20 = (f32[4,70]{1,0:T(4,128)S(1)}, f32[4,70]{1,0:T(4,128)S(1)}, u32[]{:S(2)}, u32[]{:S(2)}) collective-permute-start(f32[4,70]{1,0:T(4,128)S(1)} %broadcast_select_fusion.4), channel_id=1, source_target_pairs={{0,4},{4,8},{8,12},{12,16},{16,20},{20,24},{24,28},{28,0},{1,5},{5... | collective-permute-start | bytes 3368 | tf_op jit(solution)/shard_map/ppermute | solution.py:125
  192.1 5.4 %collective-permute-start.21 = (f32[4,70]{1,0:T(4,128)S(1)}, f32[4,70]{1,0:T(4,128)S(1)}, u32[]{:S(2)}, u32[]{:S(2)}) collective-permute-start(f32[4,70]{1,0:T(4,128)S(1)} %broadcast_select_fusion.4), channel_id=1, source_target_pairs={{0,8},{4,12},{8,16},{12,20},{16,24},{20,28},{24,0},{28,4},{1,9},{5... | collective-permute-start | bytes 3368 | tf_op jit(solution)/shard_map/ppermute | solution.py:125
  193.8 6.0 %collective-permute-start.22 = (f32[4,70]{1,0:T(4,128)S(1)}, f32[4,70]{1,0:T(4,128)S(1)}, u32[]{:S(2)}, u32[]{:S(2)}) collective-permute-start(f32[4,70]{1,0:T(4,128)S(1)} %broadcast_select_fusion.4), channel_id=1, source_target_pairs={{0,12},{4,16},{8,20},{12,24},{16,28},{20,0},{24,4},{28,8},{1,13},{... | collective-permute-start | bytes 3368 | tf_op jit(solution)/shard_map/ppermute | solution.py:125
  194.7 5.1 %collective-permute-start.23 = (f32[4,70]{1,0:T(4,128)S(1)}, f32[4,70]{1,0:T(4,128)S(1)}, u32[]{:S(2)}, u32[]{:S(2)}) collective-permute-start(f32[4,70]{1,0:T(4,128)S(1)} %broadcast_select_fusion.4), channel_id=1, source_target_pairs={{0,16},{4,20},{8,24},{12,28},{16,0},{20,4},{24,8},{28,12},{1,17},{... | collective-permute-start | bytes 3368 | tf_op jit(solution)/shard_map/ppermute | solution.py:125
  196.1 3.8 %collective-permute-start.24 = (f32[4,70]{1,0:T(4,128)S(1)}, f32[4,70]{1,0:T(4,128)S(1)}, u32[]{:S(2)}, u32[]{:S(2)}) collective-permute-start(f32[4,70]{1,0:T(4,128)S(1)} %broadcast_select_fusion.4), channel_id=1, source_target_pairs={{0,20},{4,24},{8,28},{12,0},{16,4},{20,8},{24,12},{28,16},{1,21},{... | collective-permute-start | bytes 3368 | tf_op jit(solution)/shard_map/ppermute | solution.py:125
  196.1 3.8 %collective-permute-start.25 = (f32[4,70]{1,0:T(4,128)S(1)}, f32[4,70]{1,0:T(4,128)S(1)}, u32[]{:S(2)}, u32[]{:S(2)}) collective-permute-start(f32[4,70]{1,0:T(4,128)S(1)} %broadcast_select_fusion.4), channel_id=1, source_target_pairs={{0,24},{4,28},{8,0},{12,4},{16,8},{20,12},{24,16},{28,20},{1,25},{... | collective-permute-start | bytes 3368 | tf_op jit(solution)/shard_map/ppermute | solution.py:125
  197.5 3.7 %collective-permute-start.26 = (f32[4,70]{1,0:T(4,128)S(1)}, f32[4,70]{1,0:T(4,128)S(1)}, u32[]{:S(2)}, u32[]{:S(2)}) collective-permute-start(f32[4,70]{1,0:T(4,128)S(1)} %broadcast_select_fusion.4), channel_id=1, source_target_pairs={{0,28},{4,0},{8,4},{12,8},{16,12},{20,16},{24,20},{28,24},{1,29},{... | collective-permute-start | bytes 3368 | tf_op jit(solution)/shard_map/ppermute | solution.py:125
  230.9 19.0 %copy-start.12 = (pred[4]{0:T(512)(128)(4,1)S(1)}, pred[4]{0:T(512)(128)(4,1)}, u32[]{:S(2)}) copy-start(pred[4]{0:T(512)(128)(4,1)} %copy-done.10) | copy-start | bytes 16
  240.2 6.9 %collective-permute-start.27 = (bf16[64,512]{1,0:T(8,128)(2,1)S(1)}, bf16[64,512]{1,0:T(8,128)(2,1)S(1)}, u32[]{:S(2)}, u32[]{:S(2)}) collective-permute-start(bf16[64,512]{1,0:T(8,128)(2,1)S(1)} %bitcast.212), channel_id=1, source_target_pairs={{0,1},{1,2},{2,3},{3,0},{4,5},{5,6},{6,7},{7,4},{8,9},{9,10},{10,1... | collective-permute-start | bytes 196616 | tf_op jit(solution)/shard_map/ppermute | solution.py:125
  241.1 7.8 %collective-permute-start.28 = (bf16[64,512]{1,0:T(8,128)(2,1)S(1)}, bf16[64,512]{1,0:T(8,128)(2,1)S(1)}, u32[]{:S(2)}, u32[]{:S(2)}) collective-permute-start(bf16[64,512]{1,0:T(8,128)(2,1)S(1)} %bitcast.213), channel_id=1, source_target_pairs={{0,2},{1,3},{2,0},{3,1},{4,6},{5,7},{6,4},{7,5},{8,10},{9,11},{10,... | collective-permute-start | bytes 196616 | tf_op jit(solution)/shard_map/ppermute | solution.py:125
  244.0 5.2 %collective-permute-start.29 = (bf16[64,512]{1,0:T(8,128)(2,1)S(1)}, bf16[64,512]{1,0:T(8,128)(2,1)S(1)}, u32[]{:S(2)}, u32[]{:S(2)}) collective-permute-start(bf16[64,512]{1,0:T(8,128)(2,1)S(1)} %bitcast.214), channel_id=1, source_target_pairs={{0,3},{1,0},{2,1},{3,2},{4,7},{5,4},{6,5},{7,6},{8,11},{9,8},{10,9... | collective-permute-start | bytes 196616 | tf_op jit(solution)/shard_map/ppermute | solution.py:125
  (3 other events, 4.7 us)
